TPU v7x, 256 devices: a whole 4x4x8 slice. The times are simulated.
256 devices in a mesh: lat: 16 (over y, x_lo, core), lon: 16 (over x_hi, z).
Axes of the slice: x: 4 (x_hi: 2, x_lo: 2; x = x_hi * 2 + x_lo), y: 4, z: 8, core: 2. Of those that a mesh axis runs over, the one named last changes fastest.
Arguments:
- fields: bfloat16 [64, 2048, 192], P('lat', 'lon'), may hold values from -6 to 6
- kernel_first: bfloat16 [9, 192, 192], replicated, may hold values from -0.15625 to 0.15625
- kernel_second: bfloat16 [9, 192, 192], replicated, may hold values from -0.15625 to 0.15625
- kernel_third: bfloat16 [9, 192, 192], replicated, may hold values from -0.15625 to 0.15625
- cotangent: bfloat16 [64, 2048, 192], P('lat', 'lon'), may hold values from -6 to 6
Outputs:
- output: float32 [64, 2048, 192], P('lat', 'lon')
- field_grad: float32 [64, 2048, 192], P('lat', 'lon')
- grad_first: float32 [9, 192, 192], P(None, None, 'lat')
- grad_second: float32 [9, 192, 192], P(None, None, 'lat')
- grad_third: float32 [9, 192, 192], P(None, None, 'lat')
All inputs are finite; a program needn't handle non-finite values.
Results may differ from a plain program's by a relative error of at most 0.0049.
Values may be sent and summed in bfloat16 or wider, within the bound.
No kernel may reach another device: no remote copies, remote signals or barrier semaphores. Data moves between devices by JAX's collectives and lax.ppermute only.
A program may use at most 64 MiB of HBM per device.

v0:
```python
import jax
import jax.numpy as jnp
from jax import lax
from jax.sharding import PartitionSpec as P


def exchange(x, h):
    nlat, nlon = lax.axis_size("lat"), lax.axis_size("lon")
    left = lax.ppermute(x[:, -h:], "lon", [(j, (j + 1) % nlon) for j in range(nlon)])
    right = lax.ppermute(x[:, :h], "lon", [(j, (j - 1) % nlon) for j in range(nlon)])
    x = jnp.concatenate([left, x, right], axis=1)
    top = lax.ppermute(x[-h:], "lat", [(i, i + 1) for i in range(nlat - 1)])
    bottom = lax.ppermute(x[:h], "lat", [(i + 1, i) for i in range(nlat - 1)])
    return jnp.concatenate([top, x, bottom], axis=0)


def inside(x, own_rows, h):
    first = lax.axis_index("lat") * own_rows - h
    rows = first + lax.broadcasted_iota(jnp.int32, (x.shape[0], 1, 1), 0)
    keep = (rows >= 0) & (rows < own_rows * lax.axis_size("lat"))
    return jnp.where(keep, x, jnp.zeros_like(x))


def crop(x, h):
    return x[h : x.shape[0] - h, h : x.shape[1] - h]


def gelu(z):
    return 0.5 * z * (1.0 + jax.scipy.special.erf(z * 0.7071067811865476))


def gelu_slope(z):
    return (
        0.5 * (1.0 + jax.scipy.special.erf(z * 0.7071067811865476))
        + z * jnp.exp(-0.5 * z * z) * 0.3989422804014327
    )


def forward_conv(padded, kernel):
    out_rows, out_cols = (padded.shape[0] - 2, padded.shape[1] - 2)
    total = jnp.zeros((out_rows, out_cols, kernel.shape[2]), jnp.float32)
    for tap in range(9):
        shift_a, shift_b = divmod(tap, 3)
        piece = padded[shift_a : shift_a + out_rows, shift_b : shift_b + out_cols]
        total = total + jnp.einsum(
            "rci,io->rco", piece, kernel[tap], preferred_element_type=jnp.float32
        )
    return total


def adjoint_conv(padded, kernel):
    out_rows, out_cols = (padded.shape[0] - 2, padded.shape[1] - 2)
    total = jnp.zeros((out_rows, out_cols, kernel.shape[1]), jnp.float32)
    for tap in range(9):
        shift_a, shift_b = divmod(tap, 3)
        piece = padded[2 - shift_a : 2 - shift_a + out_rows, 2 - shift_b : 2 - shift_b + out_cols]
        total = total + jnp.einsum(
            "rco,io->rci", piece, kernel[tap], preferred_element_type=jnp.float32
        )
    return total


def gray(n_bits, low):
    def label(i):
        ring = (i >> low) & ((1 << n_bits) - 1)
        return (i & ~(((1 << n_bits) - 1) << low)) | ((ring ^ (ring >> 1)) << low)
    return label


def labels(axis):
    n = lax.axis_size(axis)
    label = gray(2, 2) if axis == "lat" else gray(3, 0)
    lab = [label(i) for i in range(n)]
    pos = [0] * n
    for i, l in enumerate(lab):
        pos[l] = i
    return lab, pos


def halve(x, axis, order=None):
    n = lax.axis_size(axis)
    bits = n.bit_length() - 1
    order = tuple(range(bits)) if order is None else tuple(b for b in order if b < bits)
    lab, pos = labels(axis)
    runs, first = [], 0
    for l in range(1, n + 1):
        if l == n or pos[l] != pos[l - 1] + 1:
            runs.append(x[pos[first] : pos[l - 1] + 1])
            first = l
    x = jnp.concatenate(runs) if len(runs) > 1 else x
    me = jnp.asarray(lab, jnp.int32)[lax.axis_index(axis)]
    x = x.reshape((2,) * bits + x.shape[1:])
    left = list(range(bits - 1, -1, -1))
    for b in order:
        dim = left.index(b)
        left.remove(b)
        mine = (me >> b) & 1
        keep = lax.dynamic_index_in_dim(x, mine, dim, keepdims=False)
        send = lax.dynamic_index_in_dim(x, 1 - mine, dim, keepdims=False)
        x = keep + lax.ppermute(send, axis, [(i, pos[lab[i] ^ (1 << b)]) for i in range(n)])
    return x


def all_sum(x, axis, order=None):
    n = lax.axis_size(axis)
    lab, pos = labels(axis)
    bits = n.bit_length() - 1
    order = tuple(range(bits)) if order is None else tuple(b for b in order if b < bits)
    for b in order:
        x = x + lax.ppermute(x, axis, [(i, pos[lab[i] ^ (1 << b)]) for i in range(n)])
    return x


def kernel_grad(padded, delta, lat_order, lon_order):
    own_rows, own_cols = (delta.shape[0], delta.shape[1])
    cells = own_rows * lax.axis_size("lat") * own_cols * lax.axis_size("lon")
    scale = 1.0 / float(cells) ** 0.5
    terms = []
    for tap in range(9):
        shift_a, shift_b = divmod(tap, 3)
        piece = padded[shift_a : shift_a + own_rows, shift_b : shift_b + own_cols]
        terms.append(
            jnp.einsum("rci,rco->oi", piece, delta, preferred_element_type=jnp.float32) * scale
        )
    local_term = jnp.stack(terms, axis=1)
    n_out, taps, n_in = local_term.shape
    nlat = lax.axis_size("lat")
    owned = halve(local_term.reshape(nlat, -1, 128), "lat", lat_order)
    owned = all_sum(owned, "lon", lon_order)
    return owned.reshape(n_out // nlat, taps, n_in).transpose(1, 2, 0)


def on_device(fields, kernel_first, kernel_second, kernel_third, cotangent):
    own_rows = fields.shape[0]
    width = fields.shape[2]
    both = exchange(jnp.concatenate([fields, cotangent], axis=2), 4)
    fields_4, cotangent_3 = both[..., :width], crop(both[..., width:], 1)
    pre_first = forward_conv(fields_4, kernel_first)
    act_first = inside(gelu(pre_first).astype(jnp.bfloat16), own_rows, 3)
    pre_second = forward_conv(act_first, kernel_second)
    act_second = inside(gelu(crop(pre_second, 1)).astype(jnp.bfloat16), own_rows, 1)
    output = forward_conv(act_second, kernel_third)
    grad_third = kernel_grad(act_second, crop(cotangent_3, 3), (0, 1, 2, 3), (0, 1, 2, 3))
    delta_second = inside(
        (adjoint_conv(cotangent_3, kernel_third) * gelu_slope(pre_second)).astype(jnp.bfloat16),
        own_rows, 2,
    )
    delta_first = inside(
        (adjoint_conv(delta_second, kernel_second) * gelu_slope(crop(pre_first, 2))).astype(
            jnp.bfloat16
        ),
        own_rows, 1,
    )
    grad_second = kernel_grad(crop(act_first, 2), crop(delta_second, 2), (0, 2, 1, 3), (1, 2, 3, 0))
    field_grad = adjoint_conv(delta_first, kernel_first)
    grad_first = kernel_grad(crop(fields_4, 3), crop(delta_first, 1), (0, 3, 2, 1), (2, 3, 0, 1))
    return (output, field_grad, grad_first, grad_second, grad_third)


def solution(mesh):
    in_specs = (P("lat", "lon", None), P(), P(), P(), P("lat", "lon", None))
    out_specs = (
        P("lat", "lon", None),
        P("lat", "lon", None),
        P(None, None, "lat"),
        P(None, None, "lat"),
        P(None, None, "lat"),
    )
    return jax.shard_map(
        on_device, mesh=mesh, in_specs=in_specs, out_specs=out_specs, check_vma=False
    )
```

profile of v0, /device:TPU:4, one launch (start us, length us, event | category | flops | bytes accessed | tf_op | source)
XLA Modules:
  0.0 155.2 jit_solution(3215043103097105285)
XLA Ops:
  2.9 2.0 %collective-permute-start = (bf16[4,4,384]{2,1,0:T(4,128)(2,1)S(1)}, bf16[4,4,384]{2,1,0:T(4,128)(2,1)S(1)}, u32[]{:S(2)}, u32[]{:S(2)}) collective-permute-start(bf16[4,4,384]{2,1,0:T(4,128)(2,1)S(1)} %get-tuple-element.39), channel_id=1, source_target_pairs={{0,1},{1,2},{2,3},{3,4},{4,5},{5,6},{6,7},{7,8},{8,9},{9,10},{10,1... | collective-permute-start | bytes 36872 | tf_op jit(solution)/shard_map/ppermute | solution.py:9
  4.9 4.0 %collective-permute-start.1 = (bf16[4,4,384]{2,1,0:T(4,128)(2,1)S(1)}, bf16[4,4,384]{2,1,0:T(4,128)(2,1)S(1)}, u32[]{:S(2)}, u32[]{:S(2)}) collective-permute-start(bf16[4,4,384]{2,1,0:T(4,128)(2,1)S(1)} %get-tuple-element.40), channel_id=1, source_target_pairs={{0,15},{1,0},{2,1},{3,2},{4,3},{5,4},{6,5},{7,6},{8,7},{9,8},{10,9... | collective-permute-start | bytes 36872 | tf_op jit(solution)/shard_map/ppermute | solution.py:10
  8.8 1.6 %collective-permute-done = bf16[4,4,384]{2,1,0:T(4,128)(2,1)S(1)} collective-permute-done((bf16[4,4,384]{2,1,0:T(4,128)(2,1)S(1)}, bf16[4,4,384]{2,1,0:T(4,128)(2,1)S(1)}, u32[]{:S(2)}, u32[]{:S(2)}) %collective-permute-start) | collective-permute-done | bytes 12320 | tf_op jit(solution)/shard_map/ppermute | solution.py:9
  10.7 1.4 collective-permute-start.2
  12.1 1.5 collective-permute-start.3
  38.1 1.7 %fusion.377 = (f32[48,9,192]{0,2,1:T(8,128)}, f32[48,9,192]{0,2,1:T(8,128)}) fusion(f32[192,9,192]{0,2,1:T(8,128)S(1)} %fusion.21), kind=kLoop, calls=%fused_computation.496 | loop fusion | bytes 1327104 | tf_op jit(solution)/shard_map/slice | solution.py:88
  51.5 1.4 slice.570
  56.5 2.4 %copy.529 = f32[96,9,192]{2,1,0:T(8,128)S(1)} copy(f32[96,9,192]{0,2,1:T(8,128)} %slice.653) | data formatting | bytes 1327104 | tf_op jit(solution)/shard_map/slice | solution.py:88
  59.0 1.4 slice.576
  60.4 2.9 %copy.530 = f32[48,9,192]{2,1,0:T(8,128)} copy(f32[48,9,192]{0,2,1:T(8,128)} %get-tuple-element.25) | data formatting | bytes 663552 | tf_op jit(solution)/shard_map/slice | solution.py:88
  63.2 2.1 %slice.578 = f32[4,162,128]{2,1,0:T(8,128)} reshape(f32[48,9,192]{2,1,0:T(8,128)} %copy.530) | data formatting | bytes 663552 | tf_op jit(solution)/shard_map/slice | solution.py:88
  65.4 1.8 %copy.531 = f32[48,9,192]{2,1,0:T(8,128)} copy(f32[48,9,192]{0,2,1:T(8,128)S(1)} %copy-done.3) | data formatting | bytes 663552 | tf_op jit(solution)/shard_map/slice | solution.py:88
  67.2 2.1 %slice.580 = f32[4,162,128]{2,1,0:T(8,128)} reshape(f32[48,9,192]{2,1,0:T(8,128)} %copy.531) | data formatting | bytes 663552 | tf_op jit(solution)/shard_map/slice | solution.py:88
  73.4 7.4 %collective-permute-start.20 = (f32[2,2,2,162,128]{4,2,3,1,0:T(2,128)}, f32[2,2,2,162,128]{4,2,3,1,0:T(2,128)}, u32[]{:S(2)}, u32[]{:S(2)}) collective-permute-start(f32[2,2,2,162,128]{4,2,3,1,0:T(2,128)} %bitcast.610), channel_id=1, source_target_pairs={{0,16},{16,0},{32,48},{48,32},{64,80},{80,64},{96,112},{112,96},{1... | collective-permute-start | bytes 1990664 | tf_op jit(solution)/shard_map/ppermute | solution.py:100
  82.6 1.4 slice.554
  86.2 1.4 copy.482
  96.5 2.2 %collective-permute-start.21 = (f32[2,2,162,128]{3,2,1,0:T(8,128)S(1)}, f32[2,2,162,128]{3,2,1,0:T(8,128)S(1)}, u32[]{:S(2)}, u32[]{:S(2)}) collective-permute-start(f32[2,2,162,128]{3,2,1,0:T(8,128)S(1)} %dynamic-slice_bitcast_fusion), channel_id=1, source_target_pairs={{0,32},{16,48},{32,0},{48,16},{64,96},{80,112},{96,64},{112,80},{1... | collective-permute-start | bytes 995336 | tf_op jit(solution)/shard_map/ppermute | solution.py:100
  99.9 1.7 %collective-permute-start.13 = (f32[2,2,162,128]{3,2,1,0:T(8,128)S(1)}, f32[2,2,162,128]{3,2,1,0:T(8,128)S(1)}, u32[]{:S(2)}, u32[]{:S(2)}) collective-permute-start(f32[2,2,162,128]{3,2,1,0:T(8,128)S(1)} %dynamic-slice_bitcast_fusion.1), channel_id=1, source_target_pairs={{0,64},{16,80},{32,96},{48,112},{64,0},{80,16},{96,32},{112,48},{1... | collective-permute-start | bytes 995336 | tf_op jit(solution)/shard_map/ppermute | solution.py:100
  102.1 2.0 %collective-permute-start.5 = (f32[2,2,162,128]{3,2,1,0:T(8,128)S(1)}, f32[2,2,162,128]{3,2,1,0:T(8,128)S(1)}, u32[]{:S(2)}, u32[]{:S(2)}) collective-permute-start(f32[2,2,162,128]{3,2,1,0:T(8,128)S(1)} %bitcast.621), channel_id=1, source_target_pairs={{0,192},{16,208},{32,224},{48,240},{64,128},{80,144},{96,160},{112... | collective-permute-start | bytes 995336 | tf_op jit(solution)/shard_map/ppermute | solution.py:100
  104.1 3.2 %collective-permute-done.21 = f32[2,2,162,128]{3,2,1,0:T(8,128)S(1)} collective-permute-done((f32[2,2,162,128]{3,2,1,0:T(8,128)S(1)}, f32[2,2,162,128]{3,2,1,0:T(8,128)S(1)}, u32[]{:S(2)}, u32[]{:S(2)}) %collective-permute-start.21) | collective-permute-done | bytes 331808 | tf_op jit(solution)/shard_map/ppermute | solution.py:100
  107.4 1.7 %collective-permute-start.22 = (f32[2,162,128]{2,1,0:T(8,128)S(1)}, f32[2,162,128]{2,1,0:T(8,128)S(1)}, u32[]{:S(2)}, u32[]{:S(2)}) collective-permute-start(f32[2,162,128]{2,1,0:T(8,128)S(1)} %dynamic-slice_bitcast_fusion.2), channel_id=1, source_target_pairs={{0,64},{16,80},{32,96},{48,112},{64,0},{80,16},{96,32},{112,48},{1... | collective-permute-start | bytes 497672 | tf_op jit(solution)/shard_map/ppermute | solution.py:100
  111.0 2.3 %collective-permute-done.5 = f32[2,2,162,128]{3,2,1,0:T(8,128)S(1)} collective-permute-done((f32[2,2,162,128]{3,2,1,0:T(8,128)S(1)}, f32[2,2,162,128]{3,2,1,0:T(8,128)S(1)}, u32[]{:S(2)}, u32[]{:S(2)}) %collective-permute-start.5) | collective-permute-done | bytes 331808 | tf_op jit(solution)/shard_map/ppermute | solution.py:100
  113.8 1.9 %collective-permute-start.23 = (f32[162,128]{1,0:T(8,128)S(1)}, f32[162,128]{1,0:T(8,128)S(1)}, u32[]{:S(2)}, u32[]{:S(2)}) collective-permute-start(f32[162,128]{1,0:T(8,128)S(1)} %dynamic-slice_bitcast_fusion.5), channel_id=1, source_target_pairs={{0,192},{16,208},{32,224},{48,240},{64,128},{80,144},{96,160},{112... | collective-permute-start | bytes 248840 | tf_op jit(solution)/shard_map/ppermute | solution.py:100
  115.9 2.1 %collective-permute-start.15 = (f32[162,128]{1,0:T(8,128)S(1)}, f32[162,128]{1,0:T(8,128)S(1)}, u32[]{:S(2)}, u32[]{:S(2)}) collective-permute-start(f32[162,128]{1,0:T(8,128)S(1)} %dynamic-slice_bitcast_fusion.6), channel_id=1, source_target_pairs={{0,192},{16,208},{32,224},{48,240},{64,128},{80,144},{96,160},{112... | collective-permute-start | bytes 248840 | tf_op jit(solution)/shard_map/ppermute | solution.py:100
  121.7 4.4 %collective-permute-start.16 = (f32[162,128]{1,0:T(8,128)S(1)}, f32[162,128]{1,0:T(8,128)S(1)}, u32[]{:S(2)}, u32[]{:S(2)}) collective-permute-start(f32[162,128]{1,0:T(8,128)S(1)} %bitcast_add_fusion.10), channel_id=1, source_target_pairs={{0,3},{1,2},{2,1},{3,0},{4,7},{5,6},{6,5},{7,4},{8,11},{9,10},{10,... | collective-permute-start | bytes 248840 | tf_op jit(solution)/shard_map/ppermute | solution.py:110
  126.1 2.6 %collective-permute-start.8 = (f32[162,128]{1,0:T(8,128)S(1)}, f32[162,128]{1,0:T(8,128)S(1)}, u32[]{:S(2)}, u32[]{:S(2)}) collective-permute-start(f32[162,128]{1,0:T(8,128)S(1)} %bitcast_add_fusion.11), channel_id=1, source_target_pairs={{0,7},{1,6},{2,5},{3,4},{4,3},{5,2},{6,1},{7,0},{8,15},{9,14},{10,... | collective-permute-start | bytes 248840 | tf_op jit(solution)/shard_map/ppermute | solution.py:110
  128.9 2.0 %collective-permute-start.25 = (f32[162,128]{1,0:T(8,128)S(1)}, f32[162,128]{1,0:T(8,128)S(1)}, u32[]{:S(2)}, u32[]{:S(2)}) collective-permute-start(f32[162,128]{1,0:T(8,128)S(1)} %add.481), channel_id=1, source_target_pairs={{0,3},{1,2},{2,1},{3,0},{4,7},{5,6},{6,5},{7,4},{8,11},{9,10},{10,... | collective-permute-start | bytes 248840 | tf_op jit(solution)/shard_map/ppermute | solution.py:110
  131.0 4.9 %collective-permute-start.17 = (f32[162,128]{1,0:T(8,128)S(1)}, f32[162,128]{1,0:T(8,128)S(1)}, u32[]{:S(2)}, u32[]{:S(2)}) collective-permute-start(f32[162,128]{1,0:T(8,128)S(1)} %add.465), channel_id=1, source_target_pairs={{0,7},{1,6},{2,5},{3,4},{4,3},{5,2},{6,1},{7,0},{8,15},{9,14},{10,... | collective-permute-start | bytes 248840 | tf_op jit(solution)/shard_map/ppermute | solution.py:110
  138.8 2.2 %collective-permute-start.18 = (f32[162,128]{1,0:T(8,128)S(1)}, f32[162,128]{1,0:T(8,128)S(1)}, u32[]{:S(2)}, u32[]{:S(2)}) collective-permute-start(f32[162,128]{1,0:T(8,128)S(1)} %add.466), channel_id=1, source_target_pairs={{0,8},{1,9},{2,10},{3,11},{4,12},{5,13},{6,14},{7,15},{8,0},{9,1},... | collective-permute-start | bytes 248840 | tf_op jit(solution)/shard_map/ppermute | solution.py:110
  142.4 1.4 collective-permute-done.26
  143.8 2.8 %collective-permute-start.27 = (f32[162,128]{1,0:T(8,128)S(1)}, f32[162,128]{1,0:T(8,128)S(1)}, u32[]{:S(2)}, u32[]{:S(2)}) collective-permute-start(f32[162,128]{1,0:T(8,128)S(1)} %add.483), channel_id=1, source_target_pairs={{0,8},{1,9},{2,10},{3,11},{4,12},{5,13},{6,14},{7,15},{8,0},{9,1},... | collective-permute-start | bytes 248840 | tf_op jit(solution)/shard_map/ppermute | solution.py:110
  152.0 2.2 %collective-permute-done.11 = f32[162,128]{1,0:T(8,128)S(1)} collective-permute-done((f32[162,128]{1,0:T(8,128)S(1)}, f32[162,128]{1,0:T(8,128)S(1)}, u32[]{:S(2)}, u32[]{:S(2)}) %collective-permute-start.11) | collective-permute-done | bytes 82976 | tf_op jit(solution)/shard_map/ppermute | solution.py:110
  (233 shorter events, 75.0 us)
Async XLA Ops:
  0.6 13.0 %copy-start.22 = (s32[16]{0:T(128)S(1)}, s32[16]{0:T(128)}, u32[]{:S(2)}) copy-start(s32[16]{0:T(128)} %constant.158.clone) | copy-start | bytes 196
  2.9 7.6 %collective-permute-start = (bf16[4,4,384]{2,1,0:T(4,128)(2,1)S(1)}, bf16[4,4,384]{2,1,0:T(4,128)(2,1)S(1)}, u32[]{:S(2)}, u32[]{:S(2)}) collective-permute-start(bf16[4,4,384]{2,1,0:T(4,128)(2,1)S(1)} %get-tuple-element.39), channel_id=1, source_target_pairs={{0,1},{1,2},{2,3},{3,4},{4,5},{5,6},{6,7},{7,8},{8,9},{9,10},{10,1... | collective-permute-start | bytes 36872 | tf_op jit(solution)/shard_map/ppermute | solution.py:9
  4.9 5.6 %collective-permute-start.1 = (bf16[4,4,384]{2,1,0:T(4,128)(2,1)S(1)}, bf16[4,4,384]{2,1,0:T(4,128)(2,1)S(1)}, u32[]{:S(2)}, u32[]{:S(2)}) collective-permute-start(bf16[4,4,384]{2,1,0:T(4,128)(2,1)S(1)} %get-tuple-element.40), channel_id=1, source_target_pairs={{0,15},{1,0},{2,1},{3,2},{4,3},{5,4},{6,5},{7,6},{8,7},{9,8},{10,9... | collective-permute-start | bytes 36872 | tf_op jit(solution)/shard_map/ppermute | solution.py:10
  10.7 7.7 %copy-start = (bf16[9,192,192]{2,1,0:T(8,128)(2,1)S(1)}, bf16[9,192,192]{2,1,0:T(8,128)(2,1)}, u32[]{:S(2)}) copy-start(bf16[9,192,192]{2,1,0:T(8,128)(2,1)} %param.9) | copy-start | bytes 1990660
  10.7 6.2 %collective-permute-start.2 = (bf16[4,136,384]{2,1,0:T(8,128)(2,1)S(1)}, bf16[4,136,384]{2,1,0:T(8,128)(2,1)S(1)}, u32[]{:S(2)}, u32[]{:S(2)}) collective-permute-start(bf16[4,136,384]{2,1,0:T(8,128)(2,1)S(1)} %pad_maximum_fusion.4), channel_id=1, source_target_pairs={{0,16},{16,32},{32,48},{48,64},{64,80},{80,96},{96,112},{112,128},... | collective-permute-start | bytes 1253384 | tf_op jit(solution)/shard_map/ppermute | solution.py:12
  12.1 6.0 %collective-permute-start.3 = (bf16[4,136,384]{2,1,0:T(8,128)(2,1)S(1)}, bf16[4,136,384]{2,1,0:T(8,128)(2,1)S(1)}, u32[]{:S(2)}, u32[]{:S(2)}) collective-permute-start(bf16[4,136,384]{2,1,0:T(8,128)(2,1)S(1)} %pad_maximum_fusion.4), channel_id=1, source_target_pairs={{16,0},{32,16},{48,32},{64,48},{80,64},{96,80},{112,96},{128,112},... | collective-permute-start | bytes 1253384 | tf_op jit(solution)/shard_map/ppermute | solution.py:13
  60.4 5.0 %copy-start.3 = (f32[48,9,192]{0,2,1:T(8,128)S(1)}, f32[48,9,192]{0,2,1:T(8,128)}, u32[]{:S(2)}) copy-start(f32[48,9,192]{0,2,1:T(8,128)} %get-tuple-element.26) | copy-start | bytes 995332
  72.2 9.8 %copy-start.4 = (f32[96,9,192]{2,0,1:T(8,128)S(1)}, f32[96,9,192]{2,0,1:T(8,128)}, u32[]{:S(2)}) copy-start(f32[96,9,192]{2,0,1:T(8,128)} %slice.637) | copy-start | bytes 1990660
  73.4 21.3 %collective-permute-start.20 = (f32[2,2,2,162,128]{4,2,3,1,0:T(2,128)}, f32[2,2,2,162,128]{4,2,3,1,0:T(2,128)}, u32[]{:S(2)}, u32[]{:S(2)}) collective-permute-start(f32[2,2,2,162,128]{4,2,3,1,0:T(2,128)} %bitcast.610), channel_id=1, source_target_pairs={{0,16},{16,0},{32,48},{48,32},{64,80},{80,64},{96,112},{112,96},{1... | collective-permute-start | bytes 1990664 | tf_op jit(solution)/shard_map/ppermute | solution.py:100
  82.0 16.7 %collective-permute-start.12 = (f32[2,2,2,162,128]{4,2,3,1,0:T(2,128)}, f32[2,2,2,162,128]{4,2,3,1,0:T(2,128)}, u32[]{:S(2)}, u32[]{:S(2)}) collective-permute-start(f32[2,2,2,162,128]{4,2,3,1,0:T(2,128)} %bitcast.611), channel_id=1, source_target_pairs={{0,16},{16,0},{32,48},{48,32},{64,80},{80,64},{96,112},{112,96},{1... | collective-permute-start | bytes 1990664 | tf_op jit(solution)/shard_map/ppermute | solution.py:100
  90.2 11.3 %collective-permute-start.4 = (f32[2,2,2,162,128]{4,2,3,1,0:T(2,128)S(1)}, f32[2,2,2,162,128]{4,2,3,1,0:T(2,128)S(1)}, u32[]{:S(2)}, u32[]{:S(2)}) collective-permute-start(f32[2,2,2,162,128]{4,2,3,1,0:T(2,128)S(1)} %bitcast.620), channel_id=1, source_target_pairs={{0,16},{16,0},{32,48},{48,32},{64,80},{80,64},{96,112},{112,96},{1... | collective-permute-start | bytes 1990664 | tf_op jit(solution)/shard_map/ppermute | solution.py:100
  96.5 10.8 %collective-permute-start.21 = (f32[2,2,162,128]{3,2,1,0:T(8,128)S(1)}, f32[2,2,162,128]{3,2,1,0:T(8,128)S(1)}, u32[]{:S(2)}, u32[]{:S(2)}) collective-permute-start(f32[2,2,162,128]{3,2,1,0:T(8,128)S(1)} %dynamic-slice_bitcast_fusion), channel_id=1, source_target_pairs={{0,32},{16,48},{32,0},{48,16},{64,96},{80,112},{96,64},{112,80},{1... | collective-permute-start | bytes 995336 | tf_op jit(solution)/shard_map/ppermute | solution.py:100
  99.9 10.4 %collective-permute-start.13 = (f32[2,2,162,128]{3,2,1,0:T(8,128)S(1)}, f32[2,2,162,128]{3,2,1,0:T(8,128)S(1)}, u32[]{:S(2)}, u32[]{:S(2)}) collective-permute-start(f32[2,2,162,128]{3,2,1,0:T(8,128)S(1)} %dynamic-slice_bitcast_fusion.1), channel_id=1, source_target_pairs={{0,64},{16,80},{32,96},{48,112},{64,0},{80,16},{96,32},{112,48},{1... | collective-permute-start | bytes 995336 | tf_op jit(solution)/shard_map/ppermute | solution.py:100
  102.1 11.1 %collective-permute-start.5 = (f32[2,2,162,128]{3,2,1,0:T(8,128)S(1)}, f32[2,2,162,128]{3,2,1,0:T(8,128)S(1)}, u32[]{:S(2)}, u32[]{:S(2)}) collective-permute-start(f32[2,2,162,128]{3,2,1,0:T(8,128)S(1)} %bitcast.621), channel_id=1, source_target_pairs={{0,192},{16,208},{32,224},{48,240},{64,128},{80,144},{96,160},{112... | collective-permute-start | bytes 995336 | tf_op jit(solution)/shard_map/ppermute | solution.py:100
  107.4 6.4 %collective-permute-start.22 = (f32[2,162,128]{2,1,0:T(8,128)S(1)}, f32[2,162,128]{2,1,0:T(8,128)S(1)}, u32[]{:S(2)}, u32[]{:S(2)}) collective-permute-start(f32[2,162,128]{2,1,0:T(8,128)S(1)} %dynamic-slice_bitcast_fusion.2), channel_id=1, source_target_pairs={{0,64},{16,80},{32,96},{48,112},{64,0},{80,16},{96,32},{112,48},{1... | collective-permute-start | bytes 497672 | tf_op jit(solution)/shard_map/ppermute | solution.py:100
  110.3 5.5 %collective-permute-start.14 = (f32[2,162,128]{2,1,0:T(8,128)S(1)}, f32[2,162,128]{2,1,0:T(8,128)S(1)}, u32[]{:S(2)}, u32[]{:S(2)}) collective-permute-start(f32[2,162,128]{2,1,0:T(8,128)S(1)} %dynamic-slice_bitcast_fusion.3), channel_id=1, source_target_pairs={{0,32},{16,48},{32,0},{48,16},{64,96},{80,112},{96,64},{112,80},{1... | collective-permute-start | bytes 497672 | tf_op jit(solution)/shard_map/ppermute | solution.py:100
  113.3 5.7 %collective-permute-start.6 = (f32[2,162,128]{2,1,0:T(8,128)S(1)}, f32[2,162,128]{2,1,0:T(8,128)S(1)}, u32[]{:S(2)}, u32[]{:S(2)}) collective-permute-start(f32[2,162,128]{2,1,0:T(8,128)S(1)} %dynamic-slice_bitcast_fusion.4), channel_id=1, source_target_pairs={{0,64},{16,80},{32,96},{48,112},{64,0},{80,16},{96,32},{112,48},{1... | collective-permute-start | bytes 497672 | tf_op jit(solution)/shard_map/ppermute | solution.py:100
  113.8 6.7 %collective-permute-start.23 = (f32[162,128]{1,0:T(8,128)S(1)}, f32[162,128]{1,0:T(8,128)S(1)}, u32[]{:S(2)}, u32[]{:S(2)}) collective-permute-start(f32[162,128]{1,0:T(8,128)S(1)} %dynamic-slice_bitcast_fusion.5), channel_id=1, source_target_pairs={{0,192},{16,208},{32,224},{48,240},{64,128},{80,144},{96,160},{112... | collective-permute-start | bytes 248840 | tf_op jit(solution)/shard_map/ppermute | solution.py:100
  115.9 5.8 %collective-permute-start.15 = (f32[162,128]{1,0:T(8,128)S(1)}, f32[162,128]{1,0:T(8,128)S(1)}, u32[]{:S(2)}, u32[]{:S(2)}) collective-permute-start(f32[162,128]{1,0:T(8,128)S(1)} %dynamic-slice_bitcast_fusion.6), channel_id=1, source_target_pairs={{0,192},{16,208},{32,224},{48,240},{64,128},{80,144},{96,160},{112... | collective-permute-start | bytes 248840 | tf_op jit(solution)/shard_map/ppermute | solution.py:100
  119.1 6.9 %collective-permute-start.7 = (f32[162,128]{1,0:T(8,128)S(1)}, f32[162,128]{1,0:T(8,128)S(1)}, u32[]{:S(2)}, u32[]{:S(2)}) collective-permute-start(f32[162,128]{1,0:T(8,128)S(1)} %dynamic-slice_bitcast_fusion.7), channel_id=1, source_target_pairs={{0,32},{16,48},{32,0},{48,16},{64,96},{80,112},{96,64},{112,80},{1... | collective-permute-start | bytes 248840 | tf_op jit(solution)/shard_map/ppermute | solution.py:100
  120.5 8.4 %collective-permute-start.24 = (f32[162,128]{1,0:T(8,128)S(1)}, f32[162,128]{1,0:T(8,128)S(1)}, u32[]{:S(2)}, u32[]{:S(2)}) collective-permute-start(f32[162,128]{1,0:T(8,128)S(1)} %bitcast_add_fusion.9), channel_id=1, source_target_pairs={{0,1},{1,0},{2,3},{3,2},{4,5},{5,4},{6,7},{7,6},{8,9},{9,8},{10,11... | collective-permute-start | bytes 248840 | tf_op jit(solution)/shard_map/ppermute | solution.py:110
  121.7 9.3 %collective-permute-start.16 = (f32[162,128]{1,0:T(8,128)S(1)}, f32[162,128]{1,0:T(8,128)S(1)}, u32[]{:S(2)}, u32[]{:S(2)}) collective-permute-start(f32[162,128]{1,0:T(8,128)S(1)} %bitcast_add_fusion.10), channel_id=1, source_target_pairs={{0,3},{1,2},{2,1},{3,0},{4,7},{5,6},{6,5},{7,4},{8,11},{9,10},{10,... | collective-permute-start | bytes 248840 | tf_op jit(solution)/shard_map/ppermute | solution.py:110
  126.1 9.8 %collective-permute-start.8 = (f32[162,128]{1,0:T(8,128)S(1)}, f32[162,128]{1,0:T(8,128)S(1)}, u32[]{:S(2)}, u32[]{:S(2)}) collective-permute-start(f32[162,128]{1,0:T(8,128)S(1)} %bitcast_add_fusion.11), channel_id=1, source_target_pairs={{0,7},{1,6},{2,5},{3,4},{4,3},{5,2},{6,1},{7,0},{8,15},{9,14},{10,... | collective-permute-start | bytes 248840 | tf_op jit(solution)/shard_map/ppermute | solution.py:110
  128.9 8.1 %collective-permute-start.25 = (f32[162,128]{1,0:T(8,128)S(1)}, f32[162,128]{1,0:T(8,128)S(1)}, u32[]{:S(2)}, u32[]{:S(2)}) collective-permute-start(f32[162,128]{1,0:T(8,128)S(1)} %add.481), channel_id=1, source_target_pairs={{0,3},{1,2},{2,1},{3,0},{4,7},{5,6},{6,5},{7,4},{8,11},{9,10},{10,... | collective-permute-start | bytes 248840 | tf_op jit(solution)/shard_map/ppermute | solution.py:110
  131.0 7.8 %collective-permute-start.17 = (f32[162,128]{1,0:T(8,128)S(1)}, f32[162,128]{1,0:T(8,128)S(1)}, u32[]{:S(2)}, u32[]{:S(2)}) collective-permute-start(f32[162,128]{1,0:T(8,128)S(1)} %add.465), channel_id=1, source_target_pairs={{0,7},{1,6},{2,5},{3,4},{4,3},{5,2},{6,1},{7,0},{8,15},{9,14},{10,... | collective-permute-start | bytes 248840 | tf_op jit(solution)/shard_map/ppermute | solution.py:110
  135.9 6.1 %collective-permute-start.9 = (f32[162,128]{1,0:T(8,128)S(1)}, f32[162,128]{1,0:T(8,128)S(1)}, u32[]{:S(2)}, u32[]{:S(2)}) collective-permute-start(f32[162,128]{1,0:T(8,128)S(1)} %add.449), channel_id=1, source_target_pairs={{0,8},{1,9},{2,10},{3,11},{4,12},{5,13},{6,14},{7,15},{8,0},{9,1},... | collective-permute-start | bytes 248840 | tf_op jit(solution)/shard_map/ppermute | solution.py:110
  137.0 6.7 %collective-permute-start.26 = (f32[162,128]{1,0:T(8,128)S(1)}, f32[162,128]{1,0:T(8,128)S(1)}, u32[]{:S(2)}, u32[]{:S(2)}) collective-permute-start(f32[162,128]{1,0:T(8,128)S(1)} %add.482), channel_id=1, source_target_pairs={{0,7},{1,6},{2,5},{3,4},{4,3},{5,2},{6,1},{7,0},{8,15},{9,14},{10,... | collective-permute-start | bytes 248840 | tf_op jit(solution)/shard_map/ppermute | solution.py:110
  138.8 7.8 %collective-permute-start.18 = (f32[162,128]{1,0:T(8,128)S(1)}, f32[162,128]{1,0:T(8,128)S(1)}, u32[]{:S(2)}, u32[]{:S(2)}) collective-permute-start(f32[162,128]{1,0:T(8,128)S(1)} %add.466), channel_id=1, source_target_pairs={{0,8},{1,9},{2,10},{3,11},{4,12},{5,13},{6,14},{7,15},{8,0},{9,1},... | collective-permute-start | bytes 248840 | tf_op jit(solution)/shard_map/ppermute | solution.py:110
  141.9 5.8 %collective-permute-start.10 = (f32[162,128]{1,0:T(8,128)S(1)}, f32[162,128]{1,0:T(8,128)S(1)}, u32[]{:S(2)}, u32[]{:S(2)}) collective-permute-start(f32[162,128]{1,0:T(8,128)S(1)} %add.450), channel_id=1, source_target_pairs={{0,1},{1,0},{2,3},{3,2},{4,5},{5,4},{6,7},{7,6},{8,9},{9,8},{10,11... | collective-permute-start | bytes 248840 | tf_op jit(solution)/shard_map/ppermute | solution.py:110
  143.8 6.1 %collective-permute-start.27 = (f32[162,128]{1,0:T(8,128)S(1)}, f32[162,128]{1,0:T(8,128)S(1)}, u32[]{:S(2)}, u32[]{:S(2)}) collective-permute-start(f32[162,128]{1,0:T(8,128)S(1)} %add.483), channel_id=1, source_target_pairs={{0,8},{1,9},{2,10},{3,11},{4,12},{5,13},{6,14},{7,15},{8,0},{9,1},... | collective-permute-start | bytes 248840 | tf_op jit(solution)/shard_map/ppermute | solution.py:110
  146.6 4.6 %collective-permute-start.19 = (f32[162,128]{1,0:T(8,128)S(1)}, f32[162,128]{1,0:T(8,128)S(1)}, u32[]{:S(2)}, u32[]{:S(2)}) collective-permute-start(f32[162,128]{1,0:T(8,128)S(1)} %add.467), channel_id=1, source_target_pairs={{0,1},{1,0},{2,3},{3,2},{4,5},{5,4},{6,7},{7,6},{8,9},{9,8},{10,11... | collective-permute-start | bytes 248840 | tf_op jit(solution)/shard_map/ppermute | solution.py:110
  147.8 6.4 %collective-permute-start.11 = (f32[162,128]{1,0:T(8,128)S(1)}, f32[162,128]{1,0:T(8,128)S(1)}, u32[]{:S(2)}, u32[]{:S(2)}) collective-permute-start(f32[162,128]{1,0:T(8,128)S(1)} %add.451), channel_id=1, source_target_pairs={{0,3},{1,2},{2,1},{3,0},{4,7},{5,6},{6,5},{7,4},{8,11},{9,10},{10,... | collective-permute-start | bytes 248840 | tf_op jit(solution)/shard_map/ppermute | solution.py:110
  (19 other events, 30.7 us)
where the time goes:
time: 158 us; the launch traced here: 155 us
  starting transfers between devices  52.8 us (33%)
  local copies, waits for them, and re-layouts  43.1 us (27%)
  matrix products  29.6 us (19%)
  waiting for transfers between devices  18.7 us (12%)
  other arithmetic  6.57 us (4%)
  between operations  4.44 us (3%)
    slice x24, local copies, waits for them, and re-layouts, halve(): runs.append(x[pos[first]:pos[l - 1] + 1])  30.6 us
    ppermute x12, starting transfers between devices, all_sum(): x = x + lax.ppermute(x, axis, [(i, pos[lab[i] ^ 1 << b]) for i in range(n)])  23 us
    ppermute x12, starting transfers between devices, halve(): lax.ppermute(send, axis, [(i, pos[lab[i] ^ 1 << b]) for i in range(n)])  20.9 us
    dot_general x27, matrix products, adjoint_conv(): jnp.einsum('rco,io->rci', piece, kernel[tap], preferred_element_type=jnp....  10.8 us
    dot_general x27, matrix products, forward_conv(): jnp.einsum('rci,io->rco', piece, kernel[tap], preferred_element_type=jnp....  10.2 us
    ppermute x12, waiting for transfers between devices, halve(): lax.ppermute(send, axis, [(i, pos[lab[i] ^ 1 << b]) for i in range(n)])  9.96 us
    dot_general x27, matrix products, kernel_grad(): jnp.einsum('rci,rco->oi', piece, delta, preferred_element_type=jnp.float32)  8.54 us
    unnamed x51, local copies, waits for them, and re-layouts  7.25 us
  transfers between devices with their start and end apart: 28, of which 16 were waited for; matrix products, arithmetic and copies ran while one was open for 13% of the time, Pallas kernels for 0%

commit v1 on v0

--- a/solution.py
+++ b/solution.py
@@ -77,17 +77,23 @@
     return lab, pos
 
 
+def in_label_order(x, axis):
+    n = lax.axis_size(axis)
+    block = x.shape[0] // n
+    lab, pos = labels(axis)
+    runs, first = [], 0
+    for l in range(1, n + 1):
+        if l == n or pos[l] != pos[l - 1] + 1:
+            runs.append(x[pos[first] * block : (pos[l - 1] + 1) * block])
+            first = l
+    return jnp.concatenate(runs) if len(runs) > 1 else x
+
+
 def halve(x, axis, order=None):
     n = lax.axis_size(axis)
     bits = n.bit_length() - 1
     order = tuple(range(bits)) if order is None else tuple(b for b in order if b < bits)
     lab, pos = labels(axis)
-    runs, first = [], 0
-    for l in range(1, n + 1):
-        if l == n or pos[l] != pos[l - 1] + 1:
-            runs.append(x[pos[first] : pos[l - 1] + 1])
-            first = l
-    x = jnp.concatenate(runs) if len(runs) > 1 else x
     me = jnp.asarray(lab, jnp.int32)[lax.axis_index(axis)]
     x = x.reshape((2,) * bits + x.shape[1:])
     left = list(range(bits - 1, -1, -1))
@@ -120,7 +126,10 @@
         shift_a, shift_b = divmod(tap, 3)
         piece = padded[shift_a : shift_a + own_rows, shift_b : shift_b + own_cols]
         terms.append(
-            jnp.einsum("rci,rco->oi", piece, delta, preferred_element_type=jnp.float32) * scale
+            in_label_order(
+                jnp.einsum("rci,rco->oi", piece, delta, preferred_element_type=jnp.float32) * scale,
+                "lat",
+            )
         )
     local_term = jnp.stack(terms, axis=1)
     n_out, taps, n_in = local_term.shape

time: 158 us -> 166 us (1.051)
  other arithmetic: 6.57 us -> 11.5 us
  local copies, waits for them, and re-layouts: 43.1 us -> 45.7 us
    another operation x0 -> x6, local copies, waits for them, and re-layouts: none -> 18.9 us  [the longest x3 9.8 us: kernel_grad(): local_term = jnp.stack(terms, axis=1)]
    slice x24 -> x81, local copies, waits for them, and re-layouts: 30.6 us -> 14.4 us  [in_label_order(): runs.append(x[pos[first] * block:(pos[l - 1] + 1) * block])]
    unnamed x0 -> x24, other arithmetic: none -> 6.87 us
    squeeze x8 -> x15, local copies, waits for them, and re-layouts: 0.17 us -> 5.47 us  [halve(): send = lax.dynamic_index_in_dim(x, 1 - mine, dim, keepdims=False)]
    dynamic_slice x7 -> x0, local copies, waits for them, and re-layouts: 4.21 us -> none  [the longest x4 2.75 us: halve(): send = lax.dynamic_index_in_dim(x, 1 - mine, dim, keepdims=False)]
    concatenate x3 -> x0, other arithmetic: 2.55 us -> none  [halve(): x = jnp.concatenate(runs) if len(runs) > 1 else x]
    unnamed x51 -> x153, local copies, waits for them, and re-layouts: 7.25 us -> 6.03 us
  transfers between devices with their start and end apart: 28 -> 28, of which waited for: 16 -> 15; matrix products, arithmetic and copies ran while one was open for 13% -> 17% of each run, Pallas kernels for 0% -> 0%
where the time goes in v1:
time: 166 us; the launch traced here: 163 us
  starting transfers between devices  51.9 us (31%)
  local copies, waits for them, and re-layouts  45.7 us (28%)
  matrix products  28.5 us (17%)
  waiting for transfers between devices  20.2 us (12%)
  other arithmetic  11.5 us (7%)
  between operations  5.63 us (3%)
    ppermute x12, starting transfers between devices, all_sum(): x = x + lax.ppermute(x, axis, [(i, pos[lab[i] ^ 1 << b]) for i in range(n)])  22.4 us
    ppermute x12, starting transfers between devices, halve(): lax.ppermute(send, axis, [(i, pos[lab[i] ^ 1 << b]) for i in range(n)])  20.6 us
    slice x81, local copies, waits for them, and re-layouts, in_label_order(): runs.append(x[pos[first] * block:(pos[l - 1] + 1) * block])  14.4 us
    ppermute x12, waiting for transfers between devices, halve(): lax.ppermute(send, axis, [(i, pos[lab[i] ^ 1 << b]) for i in range(n)])  11.3 us
    dot_general x27, matrix products, adjoint_conv(): jnp.einsum('rco,io->rci', piece, kernel[tap], preferred_element_type=jnp....  10.8 us
    another operation x3, local copies, waits for them, and re-layouts, kernel_grad(): local_term = jnp.stack(terms, axis=1)  9.8 us
    dot_general x27, matrix products, forward_conv(): jnp.einsum('rci,io->rco', piece, kernel[tap], preferred_element_type=jnp....  9.53 us
    another operation x3, local copies, waits for them, and re-layouts, halve(): x = x.reshape((2,) * bits + x.shape[1:])  9.08 us
  transfers between devices with their start and end apart: 28, of which 15 were waited for; matrix products, arithmetic and copies ran while one was open for 17% of the time, Pallas kernels for 0%

profile of v1, /device:TPU:4, one launch (start us, length us, event | category | flops | bytes accessed | tf_op | source)
XLA Modules:
  0.0 163.4 jit_solution(8478747171181367187)
XLA Ops:
  2.9 2.0 %collective-permute-start = (bf16[4,4,384]{2,1,0:T(4,128)(2,1)S(1)}, bf16[4,4,384]{2,1,0:T(4,128)(2,1)S(1)}, u32[]{:S(2)}, u32[]{:S(2)}) collective-permute-start(bf16[4,4,384]{2,1,0:T(4,128)(2,1)S(1)} %get-tuple-element.30), channel_id=1, source_target_pairs={{0,1},{1,2},{2,3},{3,4},{4,5},{5,6},{6,7},{7,8},{8,9},{9,10},{10,1... | collective-permute-start | bytes 36872 | tf_op jit(solution)/shard_map/ppermute | solution.py:9
  4.9 4.0 %collective-permute-start.1 = (bf16[4,4,384]{2,1,0:T(4,128)(2,1)S(1)}, bf16[4,4,384]{2,1,0:T(4,128)(2,1)S(1)}, u32[]{:S(2)}, u32[]{:S(2)}) collective-permute-start(bf16[4,4,384]{2,1,0:T(4,128)(2,1)S(1)} %get-tuple-element.31), channel_id=1, source_target_pairs={{0,15},{1,0},{2,1},{3,2},{4,3},{5,4},{6,5},{7,6},{8,7},{9,8},{10,9... | collective-permute-start | bytes 36872 | tf_op jit(solution)/shard_map/ppermute | solution.py:10
  8.8 1.6 collective-permute-done
  10.7 1.4 collective-permute-start.2
  12.1 1.5 collective-permute-start.3
  64.7 4.2 %copy.593 = f32[192,9,192]{2,1,0:T(8,128)} copy(f32[192,9,192]{0,2,1:T(8,128)} %fusion.223) | data formatting | bytes 2654208 | tf_op jit(solution)/shard_map/stack | solution.py:134
  68.9 2.4 %reshape_reshape.11 = f32[2,2,2,2,162,128]{5,4,3,2,1,0:T(8,128)S(1)} reshape(f32[192,9,192]{2,1,0:T(8,128)} %copy.593) | data formatting | bytes 2654208 | tf_op jit(solution)/shard_map/reshape;reshape | solution.py:98
  72.9 7.9 %collective-permute-start.20 = (f32[2,2,2,162,128]{4,2,3,1,0:T(2,128)}, f32[2,2,2,162,128]{4,2,3,1,0:T(2,128)}, u32[]{:S(2)}, u32[]{:S(2)}) collective-permute-start(f32[2,2,2,162,128]{4,2,3,1,0:T(2,128)} %copy.594), channel_id=1, source_target_pairs={{0,16},{16,0},{32,48},{48,32},{64,80},{80,64},{96,112},{112,96},{1... | collective-permute-start | bytes 1990664 | tf_op jit(solution)/shard_map/ppermute | solution.py:106
  81.7 2.8 %copy.572 = f32[192,9,192]{2,1,0:T(8,128)} copy(f32[192,9,192]{2,0,1:T(8,128)S(1)} %fusion.214) | data formatting | bytes 2654208 | tf_op jit(solution)/shard_map/stack | solution.py:134
  84.5 3.3 %reshape_reshape.10 = f32[2,2,2,2,162,128]{5,4,3,2,1,0:T(8,128)} reshape(f32[192,9,192]{2,1,0:T(8,128)} %copy.572) | data formatting | bytes 2654208 | tf_op jit(solution)/shard_map/reshape;reshape | solution.py:98
  91.6 2.8 %copy.551 = f32[192,9,192]{2,1,0:T(8,128)} copy(f32[192,9,192]{2,0,1:T(8,128)S(1)} %fusion.205) | data formatting | bytes 2654208 | tf_op jit(solution)/shard_map/stack | solution.py:134
  94.4 3.3 %reshape_reshape.9 = f32[2,2,2,2,162,128]{5,4,3,2,1,0:T(8,128)} reshape(f32[192,9,192]{2,1,0:T(8,128)} %copy.551) | data formatting | bytes 2654208 | tf_op jit(solution)/shard_map/reshape;reshape | solution.py:98
  105.0 2.2 %collective-permute-start.21 = (f32[2,2,162,128]{3,2,1,0:T(8,128)S(1)}, f32[2,2,162,128]{3,2,1,0:T(8,128)S(1)}, u32[]{:S(2)}, u32[]{:S(2)}) collective-permute-start(f32[2,2,162,128]{3,2,1,0:T(8,128)S(1)} %dynamic-slice_bitcast_fusion.3), channel_id=1, source_target_pairs={{0,32},{16,48},{32,0},{48,16},{64,96},{80,112},{96,64},{112,80},{1... | collective-permute-start | bytes 995336 | tf_op jit(solution)/shard_map/ppermute | solution.py:106
  108.4 1.7 %collective-permute-start.13 = (f32[2,2,162,128]{3,2,1,0:T(8,128)S(1)}, f32[2,2,162,128]{3,2,1,0:T(8,128)S(1)}, u32[]{:S(2)}, u32[]{:S(2)}) collective-permute-start(f32[2,2,162,128]{3,2,1,0:T(8,128)S(1)} %dynamic-slice_bitcast_fusion.4), channel_id=1, source_target_pairs={{0,64},{16,80},{32,96},{48,112},{64,0},{80,16},{96,32},{112,48},{1... | collective-permute-start | bytes 995336 | tf_op jit(solution)/shard_map/ppermute | solution.py:106
  110.2 2.0 %collective-permute-start.5 = (f32[2,2,162,128]{3,2,1,0:T(8,128)S(1)}, f32[2,2,162,128]{3,2,1,0:T(8,128)S(1)}, u32[]{:S(2)}, u32[]{:S(2)}) collective-permute-start(f32[2,2,162,128]{3,2,1,0:T(8,128)S(1)} %dynamic-slice_bitcast_fusion.5), channel_id=1, source_target_pairs={{0,192},{16,208},{32,224},{48,240},{64,128},{80,144},{96,160},{112... | collective-permute-start | bytes 995336 | tf_op jit(solution)/shard_map/ppermute | solution.py:106
  112.2 3.3 %collective-permute-done.21 = f32[2,2,162,128]{3,2,1,0:T(8,128)S(1)} collective-permute-done((f32[2,2,162,128]{3,2,1,0:T(8,128)S(1)}, f32[2,2,162,128]{3,2,1,0:T(8,128)S(1)}, u32[]{:S(2)}, u32[]{:S(2)}) %collective-permute-start.21) | collective-permute-done | bytes 331808 | tf_op jit(solution)/shard_map/ppermute | solution.py:106
  115.6 1.7 %collective-permute-start.22 = (f32[2,162,128]{2,1,0:T(8,128)S(1)}, f32[2,162,128]{2,1,0:T(8,128)S(1)}, u32[]{:S(2)}, u32[]{:S(2)}) collective-permute-start(f32[2,162,128]{2,1,0:T(8,128)S(1)} %dynamic-slice_bitcast_fusion.6), channel_id=1, source_target_pairs={{0,64},{16,80},{32,96},{48,112},{64,0},{80,16},{96,32},{112,48},{1... | collective-permute-start | bytes 497672 | tf_op jit(solution)/shard_map/ppermute | solution.py:106
  117.3 1.5 collective-permute-done.13
  119.2 1.9 %collective-permute-done.5 = f32[2,2,162,128]{3,2,1,0:T(8,128)S(1)} collective-permute-done((f32[2,2,162,128]{3,2,1,0:T(8,128)S(1)}, f32[2,2,162,128]{3,2,1,0:T(8,128)S(1)}, u32[]{:S(2)}, u32[]{:S(2)}) %collective-permute-start.5) | collective-permute-done | bytes 331808 | tf_op jit(solution)/shard_map/ppermute | solution.py:106
  122.0 2.0 %collective-permute-start.23 = (f32[162,128]{1,0:T(8,128)S(1)}, f32[162,128]{1,0:T(8,128)S(1)}, u32[]{:S(2)}, u32[]{:S(2)}) collective-permute-start(f32[162,128]{1,0:T(8,128)S(1)} %dynamic-slice_bitcast_fusion.9), channel_id=1, source_target_pairs={{0,192},{16,208},{32,224},{48,240},{64,128},{80,144},{96,160},{112... | collective-permute-start | bytes 248840 | tf_op jit(solution)/shard_map/ppermute | solution.py:106
  124.4 1.6 collective-permute-start.15
  127.2 1.4 collective-permute-done.23
  128.7 1.5 collective-permute-done.15
  130.2 4.1 %collective-permute-start.16 = (f32[162,128]{1,0:T(8,128)S(1)}, f32[162,128]{1,0:T(8,128)S(1)}, u32[]{:S(2)}, u32[]{:S(2)}) collective-permute-start(f32[162,128]{1,0:T(8,128)S(1)} %bitcast_add_fusion.10), channel_id=1, source_target_pairs={{0,3},{1,2},{2,1},{3,0},{4,7},{5,6},{6,5},{7,4},{8,11},{9,10},{10,... | collective-permute-start | bytes 248840 | tf_op jit(solution)/shard_map/ppermute | solution.py:116
  134.3 1.9 %collective-permute-start.8 = (f32[162,128]{1,0:T(8,128)S(1)}, f32[162,128]{1,0:T(8,128)S(1)}, u32[]{:S(2)}, u32[]{:S(2)}) collective-permute-start(f32[162,128]{1,0:T(8,128)S(1)} %bitcast_add_fusion.11), channel_id=1, source_target_pairs={{0,7},{1,6},{2,5},{3,4},{4,3},{5,2},{6,1},{7,0},{8,15},{9,14},{10,... | collective-permute-start | bytes 248840 | tf_op jit(solution)/shard_map/ppermute | solution.py:116
  136.5 2.7 %collective-permute-start.25 = (f32[162,128]{1,0:T(8,128)S(1)}, f32[162,128]{1,0:T(8,128)S(1)}, u32[]{:S(2)}, u32[]{:S(2)}) collective-permute-start(f32[162,128]{1,0:T(8,128)S(1)} %add.481), channel_id=1, source_target_pairs={{0,3},{1,2},{2,1},{3,0},{4,7},{5,6},{6,5},{7,4},{8,11},{9,10},{10,... | collective-permute-start | bytes 248840 | tf_op jit(solution)/shard_map/ppermute | solution.py:116
  139.2 4.7 %collective-permute-start.17 = (f32[162,128]{1,0:T(8,128)S(1)}, f32[162,128]{1,0:T(8,128)S(1)}, u32[]{:S(2)}, u32[]{:S(2)}) collective-permute-start(f32[162,128]{1,0:T(8,128)S(1)} %add.465), channel_id=1, source_target_pairs={{0,7},{1,6},{2,5},{3,4},{4,3},{5,2},{6,1},{7,0},{8,15},{9,14},{10,... | collective-permute-start | bytes 248840 | tf_op jit(solution)/shard_map/ppermute | solution.py:116
  147.0 1.9 %collective-permute-start.18 = (f32[162,128]{1,0:T(8,128)S(1)}, f32[162,128]{1,0:T(8,128)S(1)}, u32[]{:S(2)}, u32[]{:S(2)}) collective-permute-start(f32[162,128]{1,0:T(8,128)S(1)} %add.466), channel_id=1, source_target_pairs={{0,8},{1,9},{2,10},{3,11},{4,12},{5,13},{6,14},{7,15},{8,0},{9,1},... | collective-permute-start | bytes 248840 | tf_op jit(solution)/shard_map/ppermute | solution.py:116
  150.5 1.6 collective-permute-done.26
  152.1 2.6 %collective-permute-start.27 = (f32[162,128]{1,0:T(8,128)S(1)}, f32[162,128]{1,0:T(8,128)S(1)}, u32[]{:S(2)}, u32[]{:S(2)}) collective-permute-start(f32[162,128]{1,0:T(8,128)S(1)} %add.483), channel_id=1, source_target_pairs={{0,8},{1,9},{2,10},{3,11},{4,12},{5,13},{6,14},{7,15},{8,0},{9,1},... | collective-permute-start | bytes 248840 | tf_op jit(solution)/shard_map/ppermute | solution.py:116
  156.0 1.3 collective-permute-start.11
  160.1 2.2 %collective-permute-done.11 = f32[162,128]{1,0:T(8,128)S(1)} collective-permute-done((f32[162,128]{1,0:T(8,128)S(1)}, f32[162,128]{1,0:T(8,128)S(1)}, u32[]{:S(2)}, u32[]{:S(2)}) %collective-permute-start.11) | collective-permute-done | bytes 82976 | tf_op jit(solution)/shard_map/ppermute | solution.py:116
  (422 shorter events, 76.8 us)
Async XLA Ops:
  0.6 13.0 %copy-start.73 = (s32[16]{0:T(128)S(1)}, s32[16]{0:T(128)}, u32[]{:S(2)}) copy-start(s32[16]{0:T(128)} %constant.158.clone) | copy-start | bytes 196
  2.9 7.6 %collective-permute-start = (bf16[4,4,384]{2,1,0:T(4,128)(2,1)S(1)}, bf16[4,4,384]{2,1,0:T(4,128)(2,1)S(1)}, u32[]{:S(2)}, u32[]{:S(2)}) collective-permute-start(bf16[4,4,384]{2,1,0:T(4,128)(2,1)S(1)} %get-tuple-element.30), channel_id=1, source_target_pairs={{0,1},{1,2},{2,3},{3,4},{4,5},{5,6},{6,7},{7,8},{8,9},{9,10},{10,1... | collective-permute-start | bytes 36872 | tf_op jit(solution)/shard_map/ppermute | solution.py:9
  4.9 5.6 %collective-permute-start.1 = (bf16[4,4,384]{2,1,0:T(4,128)(2,1)S(1)}, bf16[4,4,384]{2,1,0:T(4,128)(2,1)S(1)}, u32[]{:S(2)}, u32[]{:S(2)}) collective-permute-start(bf16[4,4,384]{2,1,0:T(4,128)(2,1)S(1)} %get-tuple-element.31), channel_id=1, source_target_pairs={{0,15},{1,0},{2,1},{3,2},{4,3},{5,4},{6,5},{7,6},{8,7},{9,8},{10,9... | collective-permute-start | bytes 36872 | tf_op jit(solution)/shard_map/ppermute | solution.py:10
  10.7 6.2 %collective-permute-start.2 = (bf16[4,136,384]{2,1,0:T(8,128)(2,1)S(1)}, bf16[4,136,384]{2,1,0:T(8,128)(2,1)S(1)}, u32[]{:S(2)}, u32[]{:S(2)}) collective-permute-start(bf16[4,136,384]{2,1,0:T(8,128)(2,1)S(1)} %pad_maximum_fusion.1), channel_id=1, source_target_pairs={{0,16},{16,32},{32,48},{48,64},{64,80},{80,96},{96,112},{112,128},... | collective-permute-start | bytes 1253384 | tf_op jit(solution)/shard_map/ppermute | solution.py:12
  12.1 6.0 %collective-permute-start.3 = (bf16[4,136,384]{2,1,0:T(8,128)(2,1)S(1)}, bf16[4,136,384]{2,1,0:T(8,128)(2,1)S(1)}, u32[]{:S(2)}, u32[]{:S(2)}) collective-permute-start(bf16[4,136,384]{2,1,0:T(8,128)(2,1)S(1)} %pad_maximum_fusion.1), channel_id=1, source_target_pairs={{16,0},{32,16},{48,32},{64,48},{80,64},{96,80},{112,96},{128,112},... | collective-permute-start | bytes 1253384 | tf_op jit(solution)/shard_map/ppermute | solution.py:13
  71.5 9.5 %slice-start.14 = ((f32[192,192]{1,0:T(8,128)}), f32[96,192]{1,0:T(8,128)S(1)}, s32[]{:S(2)}) async-start(f32[192,192]{1,0:T(8,128)} %copy-done.24), calls=%async_computation.14 | async-start | bytes 196608 | tf_op jit(solution)/shard_map/slice | solution.py:87
  71.5 9.5 %copy-start.48 = (f32[48,192]{1,0:T(8,128)S(1)}, f32[48,192]{1,0:T(8,128)}, u32[]{:S(2)}) copy-start(f32[48,192]{1,0:T(8,128)} %get-tuple-element.56) | copy-start | bytes 110596
  71.6 9.5 %copy-start.49 = (f32[48,192]{1,0:T(8,128)S(1)}, f32[48,192]{1,0:T(8,128)}, u32[]{:S(2)}) copy-start(f32[48,192]{1,0:T(8,128)} %get-tuple-element.57) | copy-start | bytes 110596
  72.9 30.8 %collective-permute-start.20 = (f32[2,2,2,162,128]{4,2,3,1,0:T(2,128)}, f32[2,2,2,162,128]{4,2,3,1,0:T(2,128)}, u32[]{:S(2)}, u32[]{:S(2)}) collective-permute-start(f32[2,2,2,162,128]{4,2,3,1,0:T(2,128)} %copy.594), channel_id=1, source_target_pairs={{0,16},{16,0},{32,48},{48,32},{64,80},{80,64},{96,112},{112,96},{1... | collective-permute-start | bytes 1990664 | tf_op jit(solution)/shard_map/ppermute | solution.py:106
  90.4 16.8 %collective-permute-start.12 = (f32[2,2,2,162,128]{4,2,3,1,0:T(2,128)}, f32[2,2,2,162,128]{4,2,3,1,0:T(2,128)}, u32[]{:S(2)}, u32[]{:S(2)}) collective-permute-start(f32[2,2,2,162,128]{4,2,3,1,0:T(2,128)} %copy.573), channel_id=1, source_target_pairs={{0,16},{16,0},{32,48},{48,32},{64,80},{80,64},{96,112},{112,96},{1... | collective-permute-start | bytes 1990664 | tf_op jit(solution)/shard_map/ppermute | solution.py:106
  99.3 10.8 %collective-permute-start.4 = (f32[2,2,2,162,128]{4,2,3,1,0:T(2,128)S(1)}, f32[2,2,2,162,128]{4,2,3,1,0:T(2,128)S(1)}, u32[]{:S(2)}, u32[]{:S(2)}) collective-permute-start(f32[2,2,2,162,128]{4,2,3,1,0:T(2,128)S(1)} %copy.552), channel_id=1, source_target_pairs={{0,16},{16,0},{32,48},{48,32},{64,80},{80,64},{96,112},{112,96},{1... | collective-permute-start | bytes 1990664 | tf_op jit(solution)/shard_map/ppermute | solution.py:106
  105.0 10.5 %collective-permute-start.21 = (f32[2,2,162,128]{3,2,1,0:T(8,128)S(1)}, f32[2,2,162,128]{3,2,1,0:T(8,128)S(1)}, u32[]{:S(2)}, u32[]{:S(2)}) collective-permute-start(f32[2,2,162,128]{3,2,1,0:T(8,128)S(1)} %dynamic-slice_bitcast_fusion.3), channel_id=1, source_target_pairs={{0,32},{16,48},{32,0},{48,16},{64,96},{80,112},{96,64},{112,80},{1... | collective-permute-start | bytes 995336 | tf_op jit(solution)/shard_map/ppermute | solution.py:106
  108.4 10.4 %collective-permute-start.13 = (f32[2,2,162,128]{3,2,1,0:T(8,128)S(1)}, f32[2,2,162,128]{3,2,1,0:T(8,128)S(1)}, u32[]{:S(2)}, u32[]{:S(2)}) collective-permute-start(f32[2,2,162,128]{3,2,1,0:T(8,128)S(1)} %dynamic-slice_bitcast_fusion.4), channel_id=1, source_target_pairs={{0,64},{16,80},{32,96},{48,112},{64,0},{80,16},{96,32},{112,48},{1... | collective-permute-start | bytes 995336 | tf_op jit(solution)/shard_map/ppermute | solution.py:106
  110.2 10.8 %collective-permute-start.5 = (f32[2,2,162,128]{3,2,1,0:T(8,128)S(1)}, f32[2,2,162,128]{3,2,1,0:T(8,128)S(1)}, u32[]{:S(2)}, u32[]{:S(2)}) collective-permute-start(f32[2,2,162,128]{3,2,1,0:T(8,128)S(1)} %dynamic-slice_bitcast_fusion.5), channel_id=1, source_target_pairs={{0,192},{16,208},{32,224},{48,240},{64,128},{80,144},{96,160},{112... | collective-permute-start | bytes 995336 | tf_op jit(solution)/shard_map/ppermute | solution.py:106
  115.6 6.4 %collective-permute-start.22 = (f32[2,162,128]{2,1,0:T(8,128)S(1)}, f32[2,162,128]{2,1,0:T(8,128)S(1)}, u32[]{:S(2)}, u32[]{:S(2)}) collective-permute-start(f32[2,162,128]{2,1,0:T(8,128)S(1)} %dynamic-slice_bitcast_fusion.6), channel_id=1, source_target_pairs={{0,64},{16,80},{32,96},{48,112},{64,0},{80,16},{96,32},{112,48},{1... | collective-permute-start | bytes 497672 | tf_op jit(solution)/shard_map/ppermute | solution.py:106
  118.9 5.5 %collective-permute-start.14 = (f32[2,162,128]{2,1,0:T(8,128)S(1)}, f32[2,162,128]{2,1,0:T(8,128)S(1)}, u32[]{:S(2)}, u32[]{:S(2)}) collective-permute-start(f32[2,162,128]{2,1,0:T(8,128)S(1)} %dynamic-slice_bitcast_fusion.7), channel_id=1, source_target_pairs={{0,32},{16,48},{32,0},{48,16},{64,96},{80,112},{96,64},{112,80},{1... | collective-permute-start | bytes 497672 | tf_op jit(solution)/shard_map/ppermute | solution.py:106
  121.1 5.5 %collective-permute-start.6 = (f32[2,162,128]{2,1,0:T(8,128)S(1)}, f32[2,162,128]{2,1,0:T(8,128)S(1)}, u32[]{:S(2)}, u32[]{:S(2)}) collective-permute-start(f32[2,162,128]{2,1,0:T(8,128)S(1)} %dynamic-slice_bitcast_fusion.8), channel_id=1, source_target_pairs={{0,64},{16,80},{32,96},{48,112},{64,0},{80,16},{96,32},{112,48},{1... | collective-permute-start | bytes 497672 | tf_op jit(solution)/shard_map/ppermute | solution.py:106
  122.0 6.5 %collective-permute-start.23 = (f32[162,128]{1,0:T(8,128)S(1)}, f32[162,128]{1,0:T(8,128)S(1)}, u32[]{:S(2)}, u32[]{:S(2)}) collective-permute-start(f32[162,128]{1,0:T(8,128)S(1)} %dynamic-slice_bitcast_fusion.9), channel_id=1, source_target_pairs={{0,192},{16,208},{32,224},{48,240},{64,128},{80,144},{96,160},{112... | collective-permute-start | bytes 248840 | tf_op jit(solution)/shard_map/ppermute | solution.py:106
  124.4 5.8 %collective-permute-start.15 = (f32[162,128]{1,0:T(8,128)S(1)}, f32[162,128]{1,0:T(8,128)S(1)}, u32[]{:S(2)}, u32[]{:S(2)}) collective-permute-start(f32[162,128]{1,0:T(8,128)S(1)} %dynamic-slice_bitcast_fusion.10), channel_id=1, source_target_pairs={{0,192},{16,208},{32,224},{48,240},{64,128},{80,144},{96,160},{112... | collective-permute-start | bytes 248840 | tf_op jit(solution)/shard_map/ppermute | solution.py:106
  126.7 7.6 %collective-permute-start.7 = (f32[162,128]{1,0:T(8,128)S(1)}, f32[162,128]{1,0:T(8,128)S(1)}, u32[]{:S(2)}, u32[]{:S(2)}) collective-permute-start(f32[162,128]{1,0:T(8,128)S(1)} %dynamic-slice_bitcast_fusion.11), channel_id=1, source_target_pairs={{0,32},{16,48},{32,0},{48,16},{64,96},{80,112},{96,64},{112,80},{1... | collective-permute-start | bytes 248840 | tf_op jit(solution)/shard_map/ppermute | solution.py:106
  128.6 7.9 %collective-permute-start.24 = (f32[162,128]{1,0:T(8,128)S(1)}, f32[162,128]{1,0:T(8,128)S(1)}, u32[]{:S(2)}, u32[]{:S(2)}) collective-permute-start(f32[162,128]{1,0:T(8,128)S(1)} %bitcast_add_fusion.9), channel_id=1, source_target_pairs={{0,1},{1,0},{2,3},{3,2},{4,5},{5,4},{6,7},{7,6},{8,9},{9,8},{10,11... | collective-permute-start | bytes 248840 | tf_op jit(solution)/shard_map/ppermute | solution.py:116
  130.2 9.0 %collective-permute-start.16 = (f32[162,128]{1,0:T(8,128)S(1)}, f32[162,128]{1,0:T(8,128)S(1)}, u32[]{:S(2)}, u32[]{:S(2)}) collective-permute-start(f32[162,128]{1,0:T(8,128)S(1)} %bitcast_add_fusion.10), channel_id=1, source_target_pairs={{0,3},{1,2},{2,1},{3,0},{4,7},{5,6},{6,5},{7,4},{8,11},{9,10},{10,... | collective-permute-start | bytes 248840 | tf_op jit(solution)/shard_map/ppermute | solution.py:116
  134.3 9.6 %collective-permute-start.8 = (f32[162,128]{1,0:T(8,128)S(1)}, f32[162,128]{1,0:T(8,128)S(1)}, u32[]{:S(2)}, u32[]{:S(2)}) collective-permute-start(f32[162,128]{1,0:T(8,128)S(1)} %bitcast_add_fusion.11), channel_id=1, source_target_pairs={{0,7},{1,6},{2,5},{3,4},{4,3},{5,2},{6,1},{7,0},{8,15},{9,14},{10,... | collective-permute-start | bytes 248840 | tf_op jit(solution)/shard_map/ppermute | solution.py:116
  136.5 8.8 %collective-permute-start.25 = (f32[162,128]{1,0:T(8,128)S(1)}, f32[162,128]{1,0:T(8,128)S(1)}, u32[]{:S(2)}, u32[]{:S(2)}) collective-permute-start(f32[162,128]{1,0:T(8,128)S(1)} %add.481), channel_id=1, source_target_pairs={{0,3},{1,2},{2,1},{3,0},{4,7},{5,6},{6,5},{7,4},{8,11},{9,10},{10,... | collective-permute-start | bytes 248840 | tf_op jit(solution)/shard_map/ppermute | solution.py:116
  139.2 7.8 %collective-permute-start.17 = (f32[162,128]{1,0:T(8,128)S(1)}, f32[162,128]{1,0:T(8,128)S(1)}, u32[]{:S(2)}, u32[]{:S(2)}) collective-permute-start(f32[162,128]{1,0:T(8,128)S(1)} %add.465), channel_id=1, source_target_pairs={{0,7},{1,6},{2,5},{3,4},{4,3},{5,2},{6,1},{7,0},{8,15},{9,14},{10,... | collective-permute-start | bytes 248840 | tf_op jit(solution)/shard_map/ppermute | solution.py:116
  144.0 6.1 %collective-permute-start.9 = (f32[162,128]{1,0:T(8,128)S(1)}, f32[162,128]{1,0:T(8,128)S(1)}, u32[]{:S(2)}, u32[]{:S(2)}) collective-permute-start(f32[162,128]{1,0:T(8,128)S(1)} %add.449), channel_id=1, source_target_pairs={{0,8},{1,9},{2,10},{3,11},{4,12},{5,13},{6,14},{7,15},{8,0},{9,1},... | collective-permute-start | bytes 248840 | tf_op jit(solution)/shard_map/ppermute | solution.py:116
  145.4 6.7 %collective-permute-start.26 = (f32[162,128]{1,0:T(8,128)S(1)}, f32[162,128]{1,0:T(8,128)S(1)}, u32[]{:S(2)}, u32[]{:S(2)}) collective-permute-start(f32[162,128]{1,0:T(8,128)S(1)} %add.482), channel_id=1, source_target_pairs={{0,7},{1,6},{2,5},{3,4},{4,3},{5,2},{6,1},{7,0},{8,15},{9,14},{10,... | collective-permute-start | bytes 248840 | tf_op jit(solution)/shard_map/ppermute | solution.py:116
  147.0 7.7 %collective-permute-start.18 = (f32[162,128]{1,0:T(8,128)S(1)}, f32[162,128]{1,0:T(8,128)S(1)}, u32[]{:S(2)}, u32[]{:S(2)}) collective-permute-start(f32[162,128]{1,0:T(8,128)S(1)} %add.466), channel_id=1, source_target_pairs={{0,8},{1,9},{2,10},{3,11},{4,12},{5,13},{6,14},{7,15},{8,0},{9,1},... | collective-permute-start | bytes 248840 | tf_op jit(solution)/shard_map/ppermute | solution.py:116
  150.1 5.9 %collective-permute-start.10 = (f32[162,128]{1,0:T(8,128)S(1)}, f32[162,128]{1,0:T(8,128)S(1)}, u32[]{:S(2)}, u32[]{:S(2)}) collective-permute-start(f32[162,128]{1,0:T(8,128)S(1)} %add.450), channel_id=1, source_target_pairs={{0,1},{1,0},{2,3},{3,2},{4,5},{5,4},{6,7},{7,6},{8,9},{9,8},{10,11... | collective-permute-start | bytes 248840 | tf_op jit(solution)/shard_map/ppermute | solution.py:116
  152.1 6.2 %collective-permute-start.27 = (f32[162,128]{1,0:T(8,128)S(1)}, f32[162,128]{1,0:T(8,128)S(1)}, u32[]{:S(2)}, u32[]{:S(2)}) collective-permute-start(f32[162,128]{1,0:T(8,128)S(1)} %add.483), channel_id=1, source_target_pairs={{0,8},{1,9},{2,10},{3,11},{4,12},{5,13},{6,14},{7,15},{8,0},{9,1},... | collective-permute-start | bytes 248840 | tf_op jit(solution)/shard_map/ppermute | solution.py:116
  154.7 4.6 %collective-permute-start.19 = (f32[162,128]{1,0:T(8,128)S(1)}, f32[162,128]{1,0:T(8,128)S(1)}, u32[]{:S(2)}, u32[]{:S(2)}) collective-permute-start(f32[162,128]{1,0:T(8,128)S(1)} %add.467), channel_id=1, source_target_pairs={{0,1},{1,0},{2,3},{3,2},{4,5},{5,4},{6,7},{7,6},{8,9},{9,8},{10,11... | collective-permute-start | bytes 248840 | tf_op jit(solution)/shard_map/ppermute | solution.py:116
  156.0 6.4 %collective-permute-start.11 = (f32[162,128]{1,0:T(8,128)S(1)}, f32[162,128]{1,0:T(8,128)S(1)}, u32[]{:S(2)}, u32[]{:S(2)}) collective-permute-start(f32[162,128]{1,0:T(8,128)S(1)} %add.451), channel_id=1, source_target_pairs={{0,3},{1,2},{2,1},{3,0},{4,7},{5,6},{6,5},{7,4},{8,11},{9,10},{10,... | collective-permute-start | bytes 248840 | tf_op jit(solution)/shard_map/ppermute | solution.py:116
  (97 other events, 347.1 us)

commit v2 on v0

--- a/solution.py
+++ b/solution.py
@@ -151,7 +151,7 @@
         ),
         own_rows, 1,
     )
-    grad_second = kernel_grad(crop(act_first, 2), crop(delta_second, 2), (0, 2, 1, 3), (1, 2, 3, 0))
+    grad_second = kernel_grad(crop(act_first, 2), crop(delta_second, 2), (0, 2, 3, 1), (1, 2, 3, 0))
     field_grad = adjoint_conv(delta_first, kernel_first)
     grad_first = kernel_grad(crop(fields_4, 3), crop(delta_first, 1), (0, 3, 2, 1), (2, 3, 0, 1))
     return (output, field_grad, grad_first, grad_second, grad_third)

time: 158 us -> 159 us (level)
  starting transfers between devices: 52.8 us -> 50.9 us
  waiting for transfers between devices: 18.7 us -> 20.5 us
    ppermute x12, starting transfers between devices: 23 us -> 20.5 us  [all_sum(): x = x + lax.ppermute(x, axis, [(i, pos[lab[i] ^ 1 << b]) for i in range(n)])]
  transfers between devices with their start and end apart: 28 -> 28, of which waited for: 16 -> 16; matrix products, arithmetic and copies ran while one was open for 13% -> 14% of each run, Pallas kernels for 0% -> 0%
where the time goes in v2:
time: 159 us; the launch traced here: 155 us
  starting transfers between devices  50.9 us (32%)
  local copies, waits for them, and re-layouts  43.1 us (27%)
  matrix products  29.6 us (19%)
  waiting for transfers between devices  20.5 us (13%)
  other arithmetic  6.99 us (4%)
  between operations  4.41 us (3%)
    slice x24, local copies, waits for them, and re-layouts, halve(): runs.append(x[pos[first]:pos[l - 1] + 1])  30.6 us
    ppermute x12, starting transfers between devices, halve(): lax.ppermute(send, axis, [(i, pos[lab[i] ^ 1 << b]) for i in range(n)])  21.5 us
    ppermute x12, starting transfers between devices, all_sum(): x = x + lax.ppermute(x, axis, [(i, pos[lab[i] ^ 1 << b]) for i in range(n)])  20.5 us
    dot_general x27, matrix products, adjoint_conv(): jnp.einsum('rco,io->rci', piece, kernel[tap], preferred_element_type=jnp....  10.8 us
    ppermute x12, waiting for transfers between devices, halve(): lax.ppermute(send, axis, [(i, pos[lab[i] ^ 1 << b]) for i in range(n)])  10.5 us
    dot_general x27, matrix products, forward_conv(): jnp.einsum('rci,io->rco', piece, kernel[tap], preferred_element_type=jnp....  10.2 us
    dot_general x27, matrix products, kernel_grad(): jnp.einsum('rci,rco->oi', piece, delta, preferred_element_type=jnp.float32)  8.54 us
    unnamed x51, local copies, waits for them, and re-layouts  7.25 us
  transfers between devices with their start and end apart: 28, of which 16 were waited for; matrix products, arithmetic and copies ran while one was open for 14% of the time, Pallas kernels for 0%

profile of v2, /device:TPU:4, one launch (start us, length us, event | category | flops | bytes accessed | tf_op | source)
XLA Modules:
  0.0 155.5 jit_solution(9518582276929385531)
XLA Ops:
  2.9 2.0 %collective-permute-start = (bf16[4,4,384]{2,1,0:T(4,128)(2,1)S(1)}, bf16[4,4,384]{2,1,0:T(4,128)(2,1)S(1)}, u32[]{:S(2)}, u32[]{:S(2)}) collective-permute-start(bf16[4,4,384]{2,1,0:T(4,128)(2,1)S(1)} %get-tuple-element.41), channel_id=1, source_target_pairs={{0,1},{1,2},{2,3},{3,4},{4,5},{5,6},{6,7},{7,8},{8,9},{9,10},{10,1... | collective-permute-start | bytes 36872 | tf_op jit(solution)/shard_map/ppermute | solution.py:9
  4.9 4.0 %collective-permute-start.1 = (bf16[4,4,384]{2,1,0:T(4,128)(2,1)S(1)}, bf16[4,4,384]{2,1,0:T(4,128)(2,1)S(1)}, u32[]{:S(2)}, u32[]{:S(2)}) collective-permute-start(bf16[4,4,384]{2,1,0:T(4,128)(2,1)S(1)} %get-tuple-element.42), channel_id=1, source_target_pairs={{0,15},{1,0},{2,1},{3,2},{4,3},{5,4},{6,5},{7,6},{8,7},{9,8},{10,9... | collective-permute-start | bytes 36872 | tf_op jit(solution)/shard_map/ppermute | solution.py:10
  8.8 1.6 %collective-permute-done = bf16[4,4,384]{2,1,0:T(4,128)(2,1)S(1)} collective-permute-done((bf16[4,4,384]{2,1,0:T(4,128)(2,1)S(1)}, bf16[4,4,384]{2,1,0:T(4,128)(2,1)S(1)}, u32[]{:S(2)}, u32[]{:S(2)}) %collective-permute-start) | collective-permute-done | bytes 12320 | tf_op jit(solution)/shard_map/ppermute | solution.py:9
  10.7 1.4 collective-permute-start.2
  12.1 1.5 collective-permute-start.3
  38.1 1.7 %fusion.377 = (f32[48,9,192]{0,2,1:T(8,128)}, f32[48,9,192]{0,2,1:T(8,128)}) fusion(f32[192,9,192]{0,2,1:T(8,128)S(1)} %fusion.21), kind=kLoop, calls=%fused_computation.498 | loop fusion | bytes 1327104 | tf_op jit(solution)/shard_map/slice | solution.py:88
  56.5 2.4 %copy.527 = f32[96,9,192]{2,1,0:T(8,128)S(1)} copy(f32[96,9,192]{0,2,1:T(8,128)} %slice.653) | data formatting | bytes 1327104 | tf_op jit(solution)/shard_map/slice | solution.py:88
  60.3 2.9 %copy.528 = f32[48,9,192]{2,1,0:T(8,128)} copy(f32[48,9,192]{0,2,1:T(8,128)} %get-tuple-element.25) | data formatting | bytes 663552 | tf_op jit(solution)/shard_map/slice | solution.py:88
  63.2 2.1 %slice.578 = f32[4,162,128]{2,1,0:T(8,128)} reshape(f32[48,9,192]{2,1,0:T(8,128)} %copy.528) | data formatting | bytes 663552 | tf_op jit(solution)/shard_map/slice | solution.py:88
  65.3 1.8 %copy.529 = f32[48,9,192]{2,1,0:T(8,128)} copy(f32[48,9,192]{0,2,1:T(8,128)S(1)} %copy-done.3) | data formatting | bytes 663552 | tf_op jit(solution)/shard_map/slice | solution.py:88
  67.1 2.1 %slice.580 = f32[4,162,128]{2,1,0:T(8,128)} reshape(f32[48,9,192]{2,1,0:T(8,128)} %copy.529) | data formatting | bytes 663552 | tf_op jit(solution)/shard_map/slice | solution.py:88
  73.4 7.4 %collective-permute-start.20 = (f32[2,2,2,162,128]{4,2,3,1,0:T(2,128)}, f32[2,2,2,162,128]{4,2,3,1,0:T(2,128)}, u32[]{:S(2)}, u32[]{:S(2)}) collective-permute-start(f32[2,2,2,162,128]{4,2,3,1,0:T(2,128)} %bitcast.610), channel_id=1, source_target_pairs={{0,16},{16,0},{32,48},{48,32},{64,80},{80,64},{96,112},{112,96},{1... | collective-permute-start | bytes 1990664 | tf_op jit(solution)/shard_map/ppermute | solution.py:100
  82.5 1.4 slice.554
  96.4 2.2 %collective-permute-start.21 = (f32[2,2,162,128]{3,2,1,0:T(8,128)S(1)}, f32[2,2,162,128]{3,2,1,0:T(8,128)S(1)}, u32[]{:S(2)}, u32[]{:S(2)}) collective-permute-start(f32[2,2,162,128]{3,2,1,0:T(8,128)S(1)} %dynamic-slice_bitcast_fusion), channel_id=1, source_target_pairs={{0,32},{16,48},{32,0},{48,16},{64,96},{80,112},{96,64},{112,80},{1... | collective-permute-start | bytes 995336 | tf_op jit(solution)/shard_map/ppermute | solution.py:100
  98.6 1.5 bitcast_add_fusion.1
  100.3 1.6 %collective-permute-start.13 = (f32[2,2,162,128]{3,2,1,0:T(8,128)S(1)}, f32[2,2,162,128]{3,2,1,0:T(8,128)S(1)}, u32[]{:S(2)}, u32[]{:S(2)}) collective-permute-start(f32[2,2,162,128]{3,2,1,0:T(8,128)S(1)} %bitcast.622), channel_id=1, source_target_pairs={{0,64},{16,80},{32,96},{48,112},{64,0},{80,16},{96,32},{112,48},{1... | collective-permute-start | bytes 995336 | tf_op jit(solution)/shard_map/ppermute | solution.py:100
  102.5 2.0 %collective-permute-start.5 = (f32[2,2,162,128]{3,2,1,0:T(8,128)S(1)}, f32[2,2,162,128]{3,2,1,0:T(8,128)S(1)}, u32[]{:S(2)}, u32[]{:S(2)}) collective-permute-start(f32[2,2,162,128]{3,2,1,0:T(8,128)S(1)} %bitcast.623), channel_id=1, source_target_pairs={{0,192},{16,208},{32,224},{48,240},{64,128},{80,144},{96,160},{112... | collective-permute-start | bytes 995336 | tf_op jit(solution)/shard_map/ppermute | solution.py:100
  104.5 2.8 %collective-permute-done.21 = f32[2,2,162,128]{3,2,1,0:T(8,128)S(1)} collective-permute-done((f32[2,2,162,128]{3,2,1,0:T(8,128)S(1)}, f32[2,2,162,128]{3,2,1,0:T(8,128)S(1)}, u32[]{:S(2)}, u32[]{:S(2)}) %collective-permute-start.21) | collective-permute-done | bytes 331808 | tf_op jit(solution)/shard_map/ppermute | solution.py:100
  107.3 1.7 %collective-permute-start.22 = (f32[2,162,128]{2,1,0:T(8,128)S(1)}, f32[2,162,128]{2,1,0:T(8,128)S(1)}, u32[]{:S(2)}, u32[]{:S(2)}) collective-permute-start(f32[2,162,128]{2,1,0:T(8,128)S(1)} %dynamic-slice_bitcast_fusion.1), channel_id=1, source_target_pairs={{0,64},{16,80},{32,96},{48,112},{64,0},{80,16},{96,32},{112,48},{1... | collective-permute-start | bytes 497672 | tf_op jit(solution)/shard_map/ppermute | solution.py:100
  109.0 2.1 %collective-permute-done.13 = f32[2,2,162,128]{3,2,1,0:T(8,128)S(1)} collective-permute-done((f32[2,2,162,128]{3,2,1,0:T(8,128)S(1)}, f32[2,2,162,128]{3,2,1,0:T(8,128)S(1)}, u32[]{:S(2)}, u32[]{:S(2)}) %collective-permute-start.13) | collective-permute-done | bytes 331808 | tf_op jit(solution)/shard_map/ppermute | solution.py:100
  111.2 1.9 %collective-permute-start.14 = (f32[2,162,128]{2,1,0:T(8,128)S(1)}, f32[2,162,128]{2,1,0:T(8,128)S(1)}, u32[]{:S(2)}, u32[]{:S(2)}) collective-permute-start(f32[2,162,128]{2,1,0:T(8,128)S(1)} %dynamic-slice_bitcast_fusion.2), channel_id=1, source_target_pairs={{0,192},{16,208},{32,224},{48,240},{64,128},{80,144},{96,160},{112... | collective-permute-start | bytes 497672 | tf_op jit(solution)/shard_map/ppermute | solution.py:100
  114.5 1.5 collective-permute-start.23
  116.0 2.5 %collective-permute-done.14 = f32[2,162,128]{2,1,0:T(8,128)S(1)} collective-permute-done((f32[2,162,128]{2,1,0:T(8,128)S(1)}, f32[2,162,128]{2,1,0:T(8,128)S(1)}, u32[]{:S(2)}, u32[]{:S(2)}) %collective-permute-start.14) | collective-permute-done | bytes 165920 | tf_op jit(solution)/shard_map/ppermute | solution.py:100
  119.3 1.6 %collective-permute-start.7 = (f32[162,128]{1,0:T(8,128)S(1)}, f32[162,128]{1,0:T(8,128)S(1)}, u32[]{:S(2)}, u32[]{:S(2)}) collective-permute-start(f32[162,128]{1,0:T(8,128)S(1)} %dynamic-slice_bitcast_fusion.6), channel_id=1, source_target_pairs={{0,32},{16,48},{32,0},{48,16},{64,96},{80,112},{96,64},{112,80},{1... | collective-permute-start | bytes 248840 | tf_op jit(solution)/shard_map/ppermute | solution.py:100
  121.0 2.2 %collective-permute-done.15 = f32[162,128]{1,0:T(8,128)S(1)} collective-permute-done((f32[162,128]{1,0:T(8,128)S(1)}, f32[162,128]{1,0:T(8,128)S(1)}, u32[]{:S(2)}, u32[]{:S(2)}) %collective-permute-start.15) | collective-permute-done | bytes 82976 | tf_op jit(solution)/shard_map/ppermute | solution.py:100
  123.2 4.3 %collective-permute-start.16 = (f32[162,128]{1,0:T(8,128)S(1)}, f32[162,128]{1,0:T(8,128)S(1)}, u32[]{:S(2)}, u32[]{:S(2)}) collective-permute-start(f32[162,128]{1,0:T(8,128)S(1)} %bitcast_add_fusion.10), channel_id=1, source_target_pairs={{0,3},{1,2},{2,1},{3,0},{4,7},{5,6},{6,5},{7,4},{8,11},{9,10},{10,... | collective-permute-start | bytes 248840 | tf_op jit(solution)/shard_map/ppermute | solution.py:110
  127.5 1.5 collective-permute-start.8
  129.3 3.1 %collective-permute-start.25 = (f32[162,128]{1,0:T(8,128)S(1)}, f32[162,128]{1,0:T(8,128)S(1)}, u32[]{:S(2)}, u32[]{:S(2)}) collective-permute-start(f32[162,128]{1,0:T(8,128)S(1)} %add.481), channel_id=1, source_target_pairs={{0,3},{1,2},{2,1},{3,0},{4,7},{5,6},{6,5},{7,4},{8,11},{9,10},{10,... | collective-permute-start | bytes 248840 | tf_op jit(solution)/shard_map/ppermute | solution.py:110
  132.4 2.2 %collective-permute-start.17 = (f32[162,128]{1,0:T(8,128)S(1)}, f32[162,128]{1,0:T(8,128)S(1)}, u32[]{:S(2)}, u32[]{:S(2)}) collective-permute-start(f32[162,128]{1,0:T(8,128)S(1)} %add.465), channel_id=1, source_target_pairs={{0,7},{1,6},{2,5},{3,4},{4,3},{5,2},{6,1},{7,0},{8,15},{9,14},{10,... | collective-permute-start | bytes 248840 | tf_op jit(solution)/shard_map/ppermute | solution.py:110
  136.7 4.0 %collective-permute-start.26 = (f32[162,128]{1,0:T(8,128)S(1)}, f32[162,128]{1,0:T(8,128)S(1)}, u32[]{:S(2)}, u32[]{:S(2)}) collective-permute-start(f32[162,128]{1,0:T(8,128)S(1)} %add.482), channel_id=1, source_target_pairs={{0,7},{1,6},{2,5},{3,4},{4,3},{5,2},{6,1},{7,0},{8,15},{9,14},{10,... | collective-permute-start | bytes 248840 | tf_op jit(solution)/shard_map/ppermute | solution.py:110
  145.2 1.7 %collective-permute-done.18 = f32[162,128]{1,0:T(8,128)S(1)} collective-permute-done((f32[162,128]{1,0:T(8,128)S(1)}, f32[162,128]{1,0:T(8,128)S(1)}, u32[]{:S(2)}, u32[]{:S(2)}) %collective-permute-start.18) | collective-permute-done | bytes 82976 | tf_op jit(solution)/shard_map/ppermute | solution.py:110
  152.3 2.1 %collective-permute-done.11 = f32[162,128]{1,0:T(8,128)S(1)} collective-permute-done((f32[162,128]{1,0:T(8,128)S(1)}, f32[162,128]{1,0:T(8,128)S(1)}, u32[]{:S(2)}, u32[]{:S(2)}) %collective-permute-start.11) | collective-permute-done | bytes 82976 | tf_op jit(solution)/shard_map/ppermute | solution.py:110
  (234 shorter events, 76.2 us)
Async XLA Ops:
  0.6 13.0 %copy-start.22 = (s32[16]{0:T(128)S(1)}, s32[16]{0:T(128)}, u32[]{:S(2)}) copy-start(s32[16]{0:T(128)} %constant.158.clone) | copy-start | bytes 196
  2.9 7.6 %collective-permute-start = (bf16[4,4,384]{2,1,0:T(4,128)(2,1)S(1)}, bf16[4,4,384]{2,1,0:T(4,128)(2,1)S(1)}, u32[]{:S(2)}, u32[]{:S(2)}) collective-permute-start(bf16[4,4,384]{2,1,0:T(4,128)(2,1)S(1)} %get-tuple-element.41), channel_id=1, source_target_pairs={{0,1},{1,2},{2,3},{3,4},{4,5},{5,6},{6,7},{7,8},{8,9},{9,10},{10,1... | collective-permute-start | bytes 36872 | tf_op jit(solution)/shard_map/ppermute | solution.py:9
  4.9 5.6 %collective-permute-start.1 = (bf16[4,4,384]{2,1,0:T(4,128)(2,1)S(1)}, bf16[4,4,384]{2,1,0:T(4,128)(2,1)S(1)}, u32[]{:S(2)}, u32[]{:S(2)}) collective-permute-start(bf16[4,4,384]{2,1,0:T(4,128)(2,1)S(1)} %get-tuple-element.42), channel_id=1, source_target_pairs={{0,15},{1,0},{2,1},{3,2},{4,3},{5,4},{6,5},{7,6},{8,7},{9,8},{10,9... | collective-permute-start | bytes 36872 | tf_op jit(solution)/shard_map/ppermute | solution.py:10
  10.7 7.7 %copy-start = (bf16[9,192,192]{2,1,0:T(8,128)(2,1)S(1)}, bf16[9,192,192]{2,1,0:T(8,128)(2,1)}, u32[]{:S(2)}) copy-start(bf16[9,192,192]{2,1,0:T(8,128)(2,1)} %param.9) | copy-start | bytes 1990660
  10.7 6.2 %collective-permute-start.2 = (bf16[4,136,384]{2,1,0:T(8,128)(2,1)S(1)}, bf16[4,136,384]{2,1,0:T(8,128)(2,1)S(1)}, u32[]{:S(2)}, u32[]{:S(2)}) collective-permute-start(bf16[4,136,384]{2,1,0:T(8,128)(2,1)S(1)} %pad_maximum_fusion.4), channel_id=1, source_target_pairs={{0,16},{16,32},{32,48},{48,64},{64,80},{80,96},{96,112},{112,128},... | collective-permute-start | bytes 1253384 | tf_op jit(solution)/shard_map/ppermute | solution.py:12
  12.1 6.0 %collective-permute-start.3 = (bf16[4,136,384]{2,1,0:T(8,128)(2,1)S(1)}, bf16[4,136,384]{2,1,0:T(8,128)(2,1)S(1)}, u32[]{:S(2)}, u32[]{:S(2)}) collective-permute-start(bf16[4,136,384]{2,1,0:T(8,128)(2,1)S(1)} %pad_maximum_fusion.4), channel_id=1, source_target_pairs={{16,0},{32,16},{48,32},{64,48},{80,64},{96,80},{112,96},{128,112},... | collective-permute-start | bytes 1253384 | tf_op jit(solution)/shard_map/ppermute | solution.py:13
  60.3 5.0 %copy-start.3 = (f32[48,9,192]{0,2,1:T(8,128)S(1)}, f32[48,9,192]{0,2,1:T(8,128)}, u32[]{:S(2)}) copy-start(f32[48,9,192]{0,2,1:T(8,128)} %get-tuple-element.26) | copy-start | bytes 995332
  72.1 9.8 %copy-start.4 = (f32[96,9,192]{2,0,1:T(8,128)S(1)}, f32[96,9,192]{2,0,1:T(8,128)}, u32[]{:S(2)}) copy-start(f32[96,9,192]{2,0,1:T(8,128)} %slice.637) | copy-start | bytes 1990660
  73.4 21.3 %collective-permute-start.20 = (f32[2,2,2,162,128]{4,2,3,1,0:T(2,128)}, f32[2,2,2,162,128]{4,2,3,1,0:T(2,128)}, u32[]{:S(2)}, u32[]{:S(2)}) collective-permute-start(f32[2,2,2,162,128]{4,2,3,1,0:T(2,128)} %bitcast.610), channel_id=1, source_target_pairs={{0,16},{16,0},{32,48},{48,32},{64,80},{80,64},{96,112},{112,96},{1... | collective-permute-start | bytes 1990664 | tf_op jit(solution)/shard_map/ppermute | solution.py:100
  81.9 16.7 %collective-permute-start.12 = (f32[2,2,2,162,128]{4,2,3,1,0:T(2,128)}, f32[2,2,2,162,128]{4,2,3,1,0:T(2,128)}, u32[]{:S(2)}, u32[]{:S(2)}) collective-permute-start(f32[2,2,2,162,128]{4,2,3,1,0:T(2,128)} %bitcast.611), channel_id=1, source_target_pairs={{0,16},{16,0},{32,48},{48,32},{64,80},{80,64},{96,112},{112,96},{1... | collective-permute-start | bytes 1990664 | tf_op jit(solution)/shard_map/ppermute | solution.py:100
  90.2 11.8 %collective-permute-start.4 = (f32[2,2,2,162,128]{4,2,3,1,0:T(2,128)S(1)}, f32[2,2,2,162,128]{4,2,3,1,0:T(2,128)S(1)}, u32[]{:S(2)}, u32[]{:S(2)}) collective-permute-start(f32[2,2,2,162,128]{4,2,3,1,0:T(2,128)S(1)} %bitcast.621), channel_id=1, source_target_pairs={{0,16},{16,0},{32,48},{48,32},{64,80},{80,64},{96,112},{112,96},{1... | collective-permute-start | bytes 1990664 | tf_op jit(solution)/shard_map/ppermute | solution.py:100
  96.4 10.8 %collective-permute-start.21 = (f32[2,2,162,128]{3,2,1,0:T(8,128)S(1)}, f32[2,2,162,128]{3,2,1,0:T(8,128)S(1)}, u32[]{:S(2)}, u32[]{:S(2)}) collective-permute-start(f32[2,2,162,128]{3,2,1,0:T(8,128)S(1)} %dynamic-slice_bitcast_fusion), channel_id=1, source_target_pairs={{0,32},{16,48},{32,0},{48,16},{64,96},{80,112},{96,64},{112,80},{1... | collective-permute-start | bytes 995336 | tf_op jit(solution)/shard_map/ppermute | solution.py:100
  100.3 10.8 %collective-permute-start.13 = (f32[2,2,162,128]{3,2,1,0:T(8,128)S(1)}, f32[2,2,162,128]{3,2,1,0:T(8,128)S(1)}, u32[]{:S(2)}, u32[]{:S(2)}) collective-permute-start(f32[2,2,162,128]{3,2,1,0:T(8,128)S(1)} %bitcast.622), channel_id=1, source_target_pairs={{0,64},{16,80},{32,96},{48,112},{64,0},{80,16},{96,32},{112,48},{1... | collective-permute-start | bytes 995336 | tf_op jit(solution)/shard_map/ppermute | solution.py:100
  102.5 11.1 %collective-permute-start.5 = (f32[2,2,162,128]{3,2,1,0:T(8,128)S(1)}, f32[2,2,162,128]{3,2,1,0:T(8,128)S(1)}, u32[]{:S(2)}, u32[]{:S(2)}) collective-permute-start(f32[2,2,162,128]{3,2,1,0:T(8,128)S(1)} %bitcast.623), channel_id=1, source_target_pairs={{0,192},{16,208},{32,224},{48,240},{64,128},{80,144},{96,160},{112... | collective-permute-start | bytes 995336 | tf_op jit(solution)/shard_map/ppermute | solution.py:100
  107.3 7.1 %collective-permute-start.22 = (f32[2,162,128]{2,1,0:T(8,128)S(1)}, f32[2,162,128]{2,1,0:T(8,128)S(1)}, u32[]{:S(2)}, u32[]{:S(2)}) collective-permute-start(f32[2,162,128]{2,1,0:T(8,128)S(1)} %dynamic-slice_bitcast_fusion.1), channel_id=1, source_target_pairs={{0,64},{16,80},{32,96},{48,112},{64,0},{80,16},{96,32},{112,48},{1... | collective-permute-start | bytes 497672 | tf_op jit(solution)/shard_map/ppermute | solution.py:100
  111.2 7.4 %collective-permute-start.14 = (f32[2,162,128]{2,1,0:T(8,128)S(1)}, f32[2,162,128]{2,1,0:T(8,128)S(1)}, u32[]{:S(2)}, u32[]{:S(2)}) collective-permute-start(f32[2,162,128]{2,1,0:T(8,128)S(1)} %dynamic-slice_bitcast_fusion.2), channel_id=1, source_target_pairs={{0,192},{16,208},{32,224},{48,240},{64,128},{80,144},{96,160},{112... | collective-permute-start | bytes 497672 | tf_op jit(solution)/shard_map/ppermute | solution.py:100
  113.7 5.5 %collective-permute-start.6 = (f32[2,162,128]{2,1,0:T(8,128)S(1)}, f32[2,162,128]{2,1,0:T(8,128)S(1)}, u32[]{:S(2)}, u32[]{:S(2)}) collective-permute-start(f32[2,162,128]{2,1,0:T(8,128)S(1)} %dynamic-slice_bitcast_fusion.3), channel_id=1, source_target_pairs={{0,64},{16,80},{32,96},{48,112},{64,0},{80,16},{96,32},{112,48},{1... | collective-permute-start | bytes 497672 | tf_op jit(solution)/shard_map/ppermute | solution.py:100
  114.5 6.3 %collective-permute-start.23 = (f32[162,128]{1,0:T(8,128)S(1)}, f32[162,128]{1,0:T(8,128)S(1)}, u32[]{:S(2)}, u32[]{:S(2)}) collective-permute-start(f32[162,128]{1,0:T(8,128)S(1)} %dynamic-slice_bitcast_fusion.4), channel_id=1, source_target_pairs={{0,192},{16,208},{32,224},{48,240},{64,128},{80,144},{96,160},{112... | collective-permute-start | bytes 248840 | tf_op jit(solution)/shard_map/ppermute | solution.py:100
  118.6 4.6 %collective-permute-start.15 = (f32[162,128]{1,0:T(8,128)S(1)}, f32[162,128]{1,0:T(8,128)S(1)}, u32[]{:S(2)}, u32[]{:S(2)}) collective-permute-start(f32[162,128]{1,0:T(8,128)S(1)} %dynamic-slice_bitcast_fusion.5), channel_id=1, source_target_pairs={{0,32},{16,48},{32,0},{48,16},{64,96},{80,112},{96,64},{112,80},{1... | collective-permute-start | bytes 248840 | tf_op jit(solution)/shard_map/ppermute | solution.py:100
  119.3 8.2 %collective-permute-start.7 = (f32[162,128]{1,0:T(8,128)S(1)}, f32[162,128]{1,0:T(8,128)S(1)}, u32[]{:S(2)}, u32[]{:S(2)}) collective-permute-start(f32[162,128]{1,0:T(8,128)S(1)} %dynamic-slice_bitcast_fusion.6), channel_id=1, source_target_pairs={{0,32},{16,48},{32,0},{48,16},{64,96},{80,112},{96,64},{112,80},{1... | collective-permute-start | bytes 248840 | tf_op jit(solution)/shard_map/ppermute | solution.py:100
  120.9 8.4 %collective-permute-start.24 = (f32[162,128]{1,0:T(8,128)S(1)}, f32[162,128]{1,0:T(8,128)S(1)}, u32[]{:S(2)}, u32[]{:S(2)}) collective-permute-start(f32[162,128]{1,0:T(8,128)S(1)} %bitcast_add_fusion.9), channel_id=1, source_target_pairs={{0,1},{1,0},{2,3},{3,2},{4,5},{5,4},{6,7},{7,6},{8,9},{9,8},{10,11... | collective-permute-start | bytes 248840 | tf_op jit(solution)/shard_map/ppermute | solution.py:110
  123.2 9.2 %collective-permute-start.16 = (f32[162,128]{1,0:T(8,128)S(1)}, f32[162,128]{1,0:T(8,128)S(1)}, u32[]{:S(2)}, u32[]{:S(2)}) collective-permute-start(f32[162,128]{1,0:T(8,128)S(1)} %bitcast_add_fusion.10), channel_id=1, source_target_pairs={{0,3},{1,2},{2,1},{3,0},{4,7},{5,6},{6,5},{7,4},{8,11},{9,10},{10,... | collective-permute-start | bytes 248840 | tf_op jit(solution)/shard_map/ppermute | solution.py:110
  127.5 7.9 %collective-permute-start.8 = (f32[162,128]{1,0:T(8,128)S(1)}, f32[162,128]{1,0:T(8,128)S(1)}, u32[]{:S(2)}, u32[]{:S(2)}) collective-permute-start(f32[162,128]{1,0:T(8,128)S(1)} %bitcast_add_fusion.11), channel_id=1, source_target_pairs={{0,7},{1,6},{2,5},{3,4},{4,3},{5,2},{6,1},{7,0},{8,15},{9,14},{10,... | collective-permute-start | bytes 248840 | tf_op jit(solution)/shard_map/ppermute | solution.py:110
  129.3 7.4 %collective-permute-start.25 = (f32[162,128]{1,0:T(8,128)S(1)}, f32[162,128]{1,0:T(8,128)S(1)}, u32[]{:S(2)}, u32[]{:S(2)}) collective-permute-start(f32[162,128]{1,0:T(8,128)S(1)} %add.481), channel_id=1, source_target_pairs={{0,3},{1,2},{2,1},{3,0},{4,7},{5,6},{6,5},{7,4},{8,11},{9,10},{10,... | collective-permute-start | bytes 248840 | tf_op jit(solution)/shard_map/ppermute | solution.py:110
  132.4 8.4 %collective-permute-start.17 = (f32[162,128]{1,0:T(8,128)S(1)}, f32[162,128]{1,0:T(8,128)S(1)}, u32[]{:S(2)}, u32[]{:S(2)}) collective-permute-start(f32[162,128]{1,0:T(8,128)S(1)} %add.465), channel_id=1, source_target_pairs={{0,7},{1,6},{2,5},{3,4},{4,3},{5,2},{6,1},{7,0},{8,15},{9,14},{10,... | collective-permute-start | bytes 248840 | tf_op jit(solution)/shard_map/ppermute | solution.py:110
  135.4 6.1 %collective-permute-start.9 = (f32[162,128]{1,0:T(8,128)S(1)}, f32[162,128]{1,0:T(8,128)S(1)}, u32[]{:S(2)}, u32[]{:S(2)}) collective-permute-start(f32[162,128]{1,0:T(8,128)S(1)} %add.449), channel_id=1, source_target_pairs={{0,8},{1,9},{2,10},{3,11},{4,12},{5,13},{6,14},{7,15},{8,0},{9,1},... | collective-permute-start | bytes 248840 | tf_op jit(solution)/shard_map/ppermute | solution.py:110
  136.7 7.4 %collective-permute-start.26 = (f32[162,128]{1,0:T(8,128)S(1)}, f32[162,128]{1,0:T(8,128)S(1)}, u32[]{:S(2)}, u32[]{:S(2)}) collective-permute-start(f32[162,128]{1,0:T(8,128)S(1)} %add.482), channel_id=1, source_target_pairs={{0,7},{1,6},{2,5},{3,4},{4,3},{5,2},{6,1},{7,0},{8,15},{9,14},{10,... | collective-permute-start | bytes 248840 | tf_op jit(solution)/shard_map/ppermute | solution.py:110
  140.8 6.1 %collective-permute-start.18 = (f32[162,128]{1,0:T(8,128)S(1)}, f32[162,128]{1,0:T(8,128)S(1)}, u32[]{:S(2)}, u32[]{:S(2)}) collective-permute-start(f32[162,128]{1,0:T(8,128)S(1)} %add.466), channel_id=1, source_target_pairs={{0,8},{1,9},{2,10},{3,11},{4,12},{5,13},{6,14},{7,15},{8,0},{9,1},... | collective-permute-start | bytes 248840 | tf_op jit(solution)/shard_map/ppermute | solution.py:110
  141.5 6.6 %collective-permute-start.10 = (f32[162,128]{1,0:T(8,128)S(1)}, f32[162,128]{1,0:T(8,128)S(1)}, u32[]{:S(2)}, u32[]{:S(2)}) collective-permute-start(f32[162,128]{1,0:T(8,128)S(1)} %add.450), channel_id=1, source_target_pairs={{0,1},{1,0},{2,3},{3,2},{4,5},{5,4},{6,7},{7,6},{8,9},{9,8},{10,11... | collective-permute-start | bytes 248840 | tf_op jit(solution)/shard_map/ppermute | solution.py:110
  144.1 6.1 %collective-permute-start.27 = (f32[162,128]{1,0:T(8,128)S(1)}, f32[162,128]{1,0:T(8,128)S(1)}, u32[]{:S(2)}, u32[]{:S(2)}) collective-permute-start(f32[162,128]{1,0:T(8,128)S(1)} %add.483), channel_id=1, source_target_pairs={{0,8},{1,9},{2,10},{3,11},{4,12},{5,13},{6,14},{7,15},{8,0},{9,1},... | collective-permute-start | bytes 248840 | tf_op jit(solution)/shard_map/ppermute | solution.py:110
  146.9 4.6 %collective-permute-start.19 = (f32[162,128]{1,0:T(8,128)S(1)}, f32[162,128]{1,0:T(8,128)S(1)}, u32[]{:S(2)}, u32[]{:S(2)}) collective-permute-start(f32[162,128]{1,0:T(8,128)S(1)} %add.467), channel_id=1, source_target_pairs={{0,1},{1,0},{2,3},{3,2},{4,5},{5,4},{6,7},{7,6},{8,9},{9,8},{10,11... | collective-permute-start | bytes 248840 | tf_op jit(solution)/shard_map/ppermute | solution.py:110
  148.0 6.4 %collective-permute-start.11 = (f32[162,128]{1,0:T(8,128)S(1)}, f32[162,128]{1,0:T(8,128)S(1)}, u32[]{:S(2)}, u32[]{:S(2)}) collective-permute-start(f32[162,128]{1,0:T(8,128)S(1)} %add.451), channel_id=1, source_target_pairs={{0,3},{1,2},{2,1},{3,0},{4,7},{5,6},{6,5},{7,4},{8,11},{9,10},{10,... | collective-permute-start | bytes 248840 | tf_op jit(solution)/shard_map/ppermute | solution.py:110
  (19 other events, 30.7 us)

commit v3 on v0

--- a/solution.py
+++ b/solution.py
@@ -140,7 +140,7 @@
     pre_second = forward_conv(act_first, kernel_second)
     act_second = inside(gelu(crop(pre_second, 1)).astype(jnp.bfloat16), own_rows, 1)
     output = forward_conv(act_second, kernel_third)
-    grad_third = kernel_grad(act_second, crop(cotangent_3, 3), (0, 1, 2, 3), (0, 1, 2, 3))
+    grad_third = kernel_grad(act_second, crop(cotangent_3, 3), (0, 3, 1, 2), (0, 1, 2, 3))
     delta_second = inside(
         (adjoint_conv(cotangent_3, kernel_third) * gelu_slope(pre_second)).astype(jnp.bfloat16),
         own_rows, 2,

time: 158 us -> 161 us (1.019)
  starting transfers between devices: 52.8 us -> 56.3 us
    ppermute x12, waiting for transfers between devices: 9.96 us -> 14.1 us  [halve(): lax.ppermute(send, axis, [(i, pos[lab[i] ^ 1 << b]) for i in range(n)])]
    ppermute x12, starting transfers between devices: 23 us -> 26.1 us  [all_sum(): x = x + lax.ppermute(x, axis, [(i, pos[lab[i] ^ 1 << b]) for i in range(n)])]
    ppermute x12, waiting for transfers between devices: 5.98 us -> 3.44 us  [all_sum(): x = x + lax.ppermute(x, axis, [(i, pos[lab[i] ^ 1 << b]) for i in range(n)])]
  transfers between devices with their start and end apart: 28 -> 28, of which waited for: 16 -> 10; matrix products, arithmetic and copies ran while one was open for 13% -> 16% of each run, Pallas kernels for 0% -> 0%
where the time goes in v3:
time: 161 us; the launch traced here: 158 us
  starting transfers between devices  56.3 us (35%)
  local copies, waits for them, and re-layouts  42.1 us (26%)
  matrix products  29.7 us (18%)
  waiting for transfers between devices  20.2 us (13%)
  other arithmetic  5.42 us (3%)
  between operations  4.45 us (3%)
    slice x24, local copies, waits for them, and re-layouts, halve(): runs.append(x[pos[first]:pos[l - 1] + 1])  31.8 us
    ppermute x12, starting transfers between devices, all_sum(): x = x + lax.ppermute(x, axis, [(i, pos[lab[i] ^ 1 << b]) for i in range(n)])  26.1 us
    ppermute x12, starting transfers between devices, halve(): lax.ppermute(send, axis, [(i, pos[lab[i] ^ 1 << b]) for i in range(n)])  21.1 us
    ppermute x12, waiting for transfers between devices, halve(): lax.ppermute(send, axis, [(i, pos[lab[i] ^ 1 << b]) for i in range(n)])  14.1 us
    dot_general x27, matrix products, adjoint_conv(): jnp.einsum('rco,io->rci', piece, kernel[tap], preferred_element_type=jnp....  11.3 us
    dot_general x27, matrix products, forward_conv(): jnp.einsum('rci,io->rco', piece, kernel[tap], preferred_element_type=jnp....  10.3 us
    dot_general x27, matrix products, kernel_grad(): jnp.einsum('rci,rco->oi', piece, delta, preferred_element_type=jnp.float32)  8.14 us
    unnamed x51, local copies, waits for them, and re-layouts  7.1 us
  transfers between devices with their start and end apart: 28, of which 10 were waited for; matrix products, arithmetic and copies ran while one was open for 16% of the time, Pallas kernels for 0%

profile of v3, /device:TPU:4, one launch (start us, length us, event | category | flops | bytes accessed | tf_op | source)
XLA Modules:
  0.0 158.3 jit_solution(1794127038768658608)
XLA Ops:
  2.9 2.0 %collective-permute-start = (bf16[4,4,384]{2,1,0:T(4,128)(2,1)S(1)}, bf16[4,4,384]{2,1,0:T(4,128)(2,1)S(1)}, u32[]{:S(2)}, u32[]{:S(2)}) collective-permute-start(bf16[4,4,384]{2,1,0:T(4,128)(2,1)S(1)} %get-tuple-element.37), channel_id=1, source_target_pairs={{0,1},{1,2},{2,3},{3,4},{4,5},{5,6},{6,7},{7,8},{8,9},{9,10},{10,1... | collective-permute-start | bytes 36872 | tf_op jit(solution)/shard_map/ppermute | solution.py:9
  4.9 4.0 %collective-permute-start.1 = (bf16[4,4,384]{2,1,0:T(4,128)(2,1)S(1)}, bf16[4,4,384]{2,1,0:T(4,128)(2,1)S(1)}, u32[]{:S(2)}, u32[]{:S(2)}) collective-permute-start(bf16[4,4,384]{2,1,0:T(4,128)(2,1)S(1)} %get-tuple-element.38), channel_id=1, source_target_pairs={{0,15},{1,0},{2,1},{3,2},{4,3},{5,4},{6,5},{7,6},{8,7},{9,8},{10,9... | collective-permute-start | bytes 36872 | tf_op jit(solution)/shard_map/ppermute | solution.py:10
  8.8 1.6 %collective-permute-done = bf16[4,4,384]{2,1,0:T(4,128)(2,1)S(1)} collective-permute-done((bf16[4,4,384]{2,1,0:T(4,128)(2,1)S(1)}, bf16[4,4,384]{2,1,0:T(4,128)(2,1)S(1)}, u32[]{:S(2)}, u32[]{:S(2)}) %collective-permute-start) | collective-permute-done | bytes 12320 | tf_op jit(solution)/shard_map/ppermute | solution.py:9
  10.7 1.4 collective-permute-start.2
  12.1 1.6 %collective-permute-start.3 = (bf16[4,136,384]{2,1,0:T(8,128)(2,1)S(1)}, bf16[4,136,384]{2,1,0:T(8,128)(2,1)S(1)}, u32[]{:S(2)}, u32[]{:S(2)}) collective-permute-start(bf16[4,136,384]{2,1,0:T(8,128)(2,1)S(1)} %pad_maximum_fusion.4), channel_id=1, source_target_pairs={{16,0},{32,16},{48,32},{64,48},{80,64},{96,80},{112,96},{128,112},... | collective-permute-start | bytes 1253384 | tf_op jit(solution)/shard_map/ppermute | solution.py:13
  29.4 1.8 %fusion.377 = (f32[48,9,192]{0,2,1:T(8,128)}, f32[48,9,192]{0,2,1:T(8,128)}) fusion(f32[192,9,192]{0,2,1:T(8,128)S(1)} %fusion.21), kind=kLoop, calls=%fused_computation.495 | loop fusion | bytes 1327104 | tf_op jit(solution)/shard_map/slice | solution.py:88
  51.6 2.4 %copy.526 = f32[96,9,192]{2,1,0:T(8,128)S(1)} copy(f32[96,9,192]{0,2,1:T(8,128)} %slice.653) | data formatting | bytes 1327104 | tf_op jit(solution)/shard_map/slice | solution.py:88
  55.5 2.9 %copy.527 = f32[48,9,192]{2,1,0:T(8,128)} copy(f32[48,9,192]{0,2,1:T(8,128)} %get-tuple-element.25) | data formatting | bytes 663552 | tf_op jit(solution)/shard_map/slice | solution.py:88
  58.4 2.1 %slice.578 = f32[4,162,128]{2,1,0:T(8,128)} reshape(f32[48,9,192]{2,1,0:T(8,128)} %copy.527) | data formatting | bytes 663552 | tf_op jit(solution)/shard_map/slice | solution.py:88
  60.5 1.7 %copy.528 = f32[48,9,192]{2,1,0:T(8,128)} copy(f32[48,9,192]{0,2,1:T(8,128)S(1)} %copy-done.5) | data formatting | bytes 663552 | tf_op jit(solution)/shard_map/slice | solution.py:88
  62.1 1.4 slice.580
  65.9 7.5 %collective-permute-start.20 = (f32[2,2,2,162,128]{4,2,3,1,0:T(2,128)}, f32[2,2,2,162,128]{4,2,3,1,0:T(2,128)}, u32[]{:S(2)}, u32[]{:S(2)}) collective-permute-start(f32[2,2,2,162,128]{4,2,3,1,0:T(2,128)} %bitcast.610), channel_id=1, source_target_pairs={{0,16},{16,0},{32,48},{48,32},{64,80},{80,64},{96,112},{112,96},{1... | collective-permute-start | bytes 1990664 | tf_op jit(solution)/shard_map/ppermute | solution.py:100
  74.0 1.4 slice.554
  79.0 1.7 %copy.502 = f32[96,9,192]{2,1,0:T(8,128)S(1)} copy(f32[96,9,192]{2,0,1:T(8,128)} %slice.650) | data formatting | bytes 1327104 | tf_op jit(solution)/shard_map/slice | solution.py:88
  95.8 2.2 %collective-permute-start.21 = (f32[2,2,162,128]{3,2,1,0:T(8,128)S(1)}, f32[2,2,162,128]{3,2,1,0:T(8,128)S(1)}, u32[]{:S(2)}, u32[]{:S(2)}) collective-permute-start(f32[2,2,162,128]{3,2,1,0:T(8,128)S(1)} %dynamic-slice_bitcast_fusion), channel_id=1, source_target_pairs={{0,192},{16,208},{32,224},{48,240},{64,128},{80,144},{96,160},{112... | collective-permute-start | bytes 995336 | tf_op jit(solution)/shard_map/ppermute | solution.py:100
  99.5 1.4 collective-permute-start.5
  101.0 7.1 %collective-permute-done.21 = f32[2,2,162,128]{3,2,1,0:T(8,128)S(1)} collective-permute-done((f32[2,2,162,128]{3,2,1,0:T(8,128)S(1)}, f32[2,2,162,128]{3,2,1,0:T(8,128)S(1)}, u32[]{:S(2)}, u32[]{:S(2)}) %collective-permute-start.21) | collective-permute-done | bytes 331808 | tf_op jit(solution)/shard_map/ppermute | solution.py:100
  108.1 2.2 %collective-permute-start.22 = (f32[2,162,128]{2,1,0:T(8,128)S(1)}, f32[2,162,128]{2,1,0:T(8,128)S(1)}, u32[]{:S(2)}, u32[]{:S(2)}) collective-permute-start(f32[2,162,128]{2,1,0:T(8,128)S(1)} %dynamic-slice_bitcast_fusion.2), channel_id=1, source_target_pairs={{0,32},{16,48},{32,0},{48,16},{64,96},{80,112},{96,64},{112,80},{1... | collective-permute-start | bytes 497672 | tf_op jit(solution)/shard_map/ppermute | solution.py:100
  110.7 4.1 %collective-permute-done.5 = f32[2,2,162,128]{3,2,1,0:T(8,128)S(1)} collective-permute-done((f32[2,2,162,128]{3,2,1,0:T(8,128)S(1)}, f32[2,2,162,128]{3,2,1,0:T(8,128)S(1)}, u32[]{:S(2)}, u32[]{:S(2)}) %collective-permute-start.5) | collective-permute-done | bytes 331808 | tf_op jit(solution)/shard_map/ppermute | solution.py:100
  115.6 1.6 collective-permute-start.23
  117.5 1.7 %collective-permute-start.15 = (f32[162,128]{1,0:T(8,128)S(1)}, f32[162,128]{1,0:T(8,128)S(1)}, u32[]{:S(2)}, u32[]{:S(2)}) collective-permute-start(f32[162,128]{1,0:T(8,128)S(1)} %dynamic-slice_bitcast_fusion.6), channel_id=1, source_target_pairs={{0,192},{16,208},{32,224},{48,240},{64,128},{80,144},{96,160},{112... | collective-permute-start | bytes 248840 | tf_op jit(solution)/shard_map/ppermute | solution.py:100
  119.2 2.5 %collective-permute-done.6 = f32[2,162,128]{2,1,0:T(8,128)S(1)} collective-permute-done((f32[2,162,128]{2,1,0:T(8,128)S(1)}, f32[2,162,128]{2,1,0:T(8,128)S(1)}, u32[]{:S(2)}, u32[]{:S(2)}) %collective-permute-start.6) | collective-permute-done | bytes 165920 | tf_op jit(solution)/shard_map/ppermute | solution.py:100
  121.7 2.2 %collective-permute-start.7 = (f32[162,128]{1,0:T(8,128)S(1)}, f32[162,128]{1,0:T(8,128)S(1)}, u32[]{:S(2)}, u32[]{:S(2)}) collective-permute-start(f32[162,128]{1,0:T(8,128)S(1)} %dynamic-slice_bitcast_fusion.7), channel_id=1, source_target_pairs={{0,32},{16,48},{32,0},{48,16},{64,96},{80,112},{96,64},{112,80},{1... | collective-permute-start | bytes 248840 | tf_op jit(solution)/shard_map/ppermute | solution.py:100
  124.1 4.4 %collective-permute-start.16 = (f32[162,128]{1,0:T(8,128)S(1)}, f32[162,128]{1,0:T(8,128)S(1)}, u32[]{:S(2)}, u32[]{:S(2)}) collective-permute-start(f32[162,128]{1,0:T(8,128)S(1)} %bitcast_add_fusion.10), channel_id=1, source_target_pairs={{0,3},{1,2},{2,1},{3,0},{4,7},{5,6},{6,5},{7,4},{8,11},{9,10},{10,... | collective-permute-start | bytes 248840 | tf_op jit(solution)/shard_map/ppermute | solution.py:110
  128.4 3.7 %collective-permute-start.8 = (f32[162,128]{1,0:T(8,128)S(1)}, f32[162,128]{1,0:T(8,128)S(1)}, u32[]{:S(2)}, u32[]{:S(2)}) collective-permute-start(f32[162,128]{1,0:T(8,128)S(1)} %bitcast_add_fusion.11), channel_id=1, source_target_pairs={{0,7},{1,6},{2,5},{3,4},{4,3},{5,2},{6,1},{7,0},{8,15},{9,14},{10,... | collective-permute-start | bytes 248840 | tf_op jit(solution)/shard_map/ppermute | solution.py:110
  133.3 3.2 %collective-permute-start.17 = (f32[162,128]{1,0:T(8,128)S(1)}, f32[162,128]{1,0:T(8,128)S(1)}, u32[]{:S(2)}, u32[]{:S(2)}) collective-permute-start(f32[162,128]{1,0:T(8,128)S(1)} %add.464), channel_id=1, source_target_pairs={{0,7},{1,6},{2,5},{3,4},{4,3},{5,2},{6,1},{7,0},{8,15},{9,14},{10,... | collective-permute-start | bytes 248840 | tf_op jit(solution)/shard_map/ppermute | solution.py:110
  138.9 3.2 %collective-permute-start.26 = (f32[162,128]{1,0:T(8,128)S(1)}, f32[162,128]{1,0:T(8,128)S(1)}, u32[]{:S(2)}, u32[]{:S(2)}) collective-permute-start(f32[162,128]{1,0:T(8,128)S(1)} %add.481), channel_id=1, source_target_pairs={{0,7},{1,6},{2,5},{3,4},{4,3},{5,2},{6,1},{7,0},{8,15},{9,14},{10,... | collective-permute-start | bytes 248840 | tf_op jit(solution)/shard_map/ppermute | solution.py:110
  142.1 2.1 %collective-permute-start.18 = (f32[162,128]{1,0:T(8,128)S(1)}, f32[162,128]{1,0:T(8,128)S(1)}, u32[]{:S(2)}, u32[]{:S(2)}) collective-permute-start(f32[162,128]{1,0:T(8,128)S(1)} %add.465), channel_id=1, source_target_pairs={{0,8},{1,9},{2,10},{3,11},{4,12},{5,13},{6,14},{7,15},{8,0},{9,1},... | collective-permute-start | bytes 248840 | tf_op jit(solution)/shard_map/ppermute | solution.py:110
  145.4 2.2 %collective-permute-start.27 = (f32[162,128]{1,0:T(8,128)S(1)}, f32[162,128]{1,0:T(8,128)S(1)}, u32[]{:S(2)}, u32[]{:S(2)}) collective-permute-start(f32[162,128]{1,0:T(8,128)S(1)} %add.482), channel_id=1, source_target_pairs={{0,8},{1,9},{2,10},{3,11},{4,12},{5,13},{6,14},{7,15},{8,0},{9,1},... | collective-permute-start | bytes 248840 | tf_op jit(solution)/shard_map/ppermute | solution.py:110
  148.2 2.6 %collective-permute-start.19 = (f32[162,128]{1,0:T(8,128)S(1)}, f32[162,128]{1,0:T(8,128)S(1)}, u32[]{:S(2)}, u32[]{:S(2)}) collective-permute-start(f32[162,128]{1,0:T(8,128)S(1)} %add.466), channel_id=1, source_target_pairs={{0,1},{1,0},{2,3},{3,2},{4,5},{5,4},{6,7},{7,6},{8,9},{9,8},{10,11... | collective-permute-start | bytes 248840 | tf_op jit(solution)/shard_map/ppermute | solution.py:110
  150.8 1.6 collective-permute-start.11
  155.1 2.1 %collective-permute-done.11 = f32[162,128]{1,0:T(8,128)S(1)} collective-permute-done((f32[162,128]{1,0:T(8,128)S(1)}, f32[162,128]{1,0:T(8,128)S(1)}, u32[]{:S(2)}, u32[]{:S(2)}) %collective-permute-start.11) | collective-permute-done | bytes 82976 | tf_op jit(solution)/shard_map/ppermute | solution.py:110
  (233 shorter events, 70.3 us)
Async XLA Ops:
  0.6 13.1 %copy-start.22 = (s32[16]{0:T(128)S(1)}, s32[16]{0:T(128)}, u32[]{:S(2)}) copy-start(s32[16]{0:T(128)} %constant.156.clone) | copy-start | bytes 196
  2.9 7.6 %collective-permute-start = (bf16[4,4,384]{2,1,0:T(4,128)(2,1)S(1)}, bf16[4,4,384]{2,1,0:T(4,128)(2,1)S(1)}, u32[]{:S(2)}, u32[]{:S(2)}) collective-permute-start(bf16[4,4,384]{2,1,0:T(4,128)(2,1)S(1)} %get-tuple-element.37), channel_id=1, source_target_pairs={{0,1},{1,2},{2,3},{3,4},{4,5},{5,6},{6,7},{7,8},{8,9},{9,10},{10,1... | collective-permute-start | bytes 36872 | tf_op jit(solution)/shard_map/ppermute | solution.py:9
  4.9 5.6 %collective-permute-start.1 = (bf16[4,4,384]{2,1,0:T(4,128)(2,1)S(1)}, bf16[4,4,384]{2,1,0:T(4,128)(2,1)S(1)}, u32[]{:S(2)}, u32[]{:S(2)}) collective-permute-start(bf16[4,4,384]{2,1,0:T(4,128)(2,1)S(1)} %get-tuple-element.38), channel_id=1, source_target_pairs={{0,15},{1,0},{2,1},{3,2},{4,3},{5,4},{6,5},{7,6},{8,7},{9,8},{10,9... | collective-permute-start | bytes 36872 | tf_op jit(solution)/shard_map/ppermute | solution.py:10
  10.7 7.7 %copy-start.2 = (bf16[9,192,192]{2,1,0:T(8,128)(2,1)S(1)}, bf16[9,192,192]{2,1,0:T(8,128)(2,1)}, u32[]{:S(2)}) copy-start(bf16[9,192,192]{2,1,0:T(8,128)(2,1)} %param.9) | copy-start | bytes 1990660
  10.7 6.3 %collective-permute-start.2 = (bf16[4,136,384]{2,1,0:T(8,128)(2,1)S(1)}, bf16[4,136,384]{2,1,0:T(8,128)(2,1)S(1)}, u32[]{:S(2)}, u32[]{:S(2)}) collective-permute-start(bf16[4,136,384]{2,1,0:T(8,128)(2,1)S(1)} %pad_maximum_fusion.4), channel_id=1, source_target_pairs={{0,16},{16,32},{32,48},{48,64},{64,80},{80,96},{96,112},{112,128},... | collective-permute-start | bytes 1253384 | tf_op jit(solution)/shard_map/ppermute | solution.py:12
  12.1 6.0 %collective-permute-start.3 = (bf16[4,136,384]{2,1,0:T(8,128)(2,1)S(1)}, bf16[4,136,384]{2,1,0:T(8,128)(2,1)S(1)}, u32[]{:S(2)}, u32[]{:S(2)}) collective-permute-start(bf16[4,136,384]{2,1,0:T(8,128)(2,1)S(1)} %pad_maximum_fusion.4), channel_id=1, source_target_pairs={{16,0},{32,16},{48,32},{64,48},{80,64},{96,80},{112,96},{128,112},... | collective-permute-start | bytes 1253384 | tf_op jit(solution)/shard_map/ppermute | solution.py:13
  55.4 5.0 %copy-start.5 = (f32[48,9,192]{0,2,1:T(8,128)S(1)}, f32[48,9,192]{0,2,1:T(8,128)}, u32[]{:S(2)}) copy-start(f32[48,9,192]{0,2,1:T(8,128)} %get-tuple-element.26) | copy-start | bytes 995332
  64.6 8.9 %copy-start.6 = (f32[96,9,192]{2,0,1:T(8,128)S(1)}, f32[96,9,192]{2,0,1:T(8,128)}, u32[]{:S(2)}) copy-start(f32[96,9,192]{2,0,1:T(8,128)} %slice.637) | copy-start | bytes 1990660
  65.9 27.9 %collective-permute-start.20 = (f32[2,2,2,162,128]{4,2,3,1,0:T(2,128)}, f32[2,2,2,162,128]{4,2,3,1,0:T(2,128)}, u32[]{:S(2)}, u32[]{:S(2)}) collective-permute-start(f32[2,2,2,162,128]{4,2,3,1,0:T(2,128)} %bitcast.610), channel_id=1, source_target_pairs={{0,16},{16,0},{32,48},{48,32},{64,80},{80,64},{96,112},{112,96},{1... | collective-permute-start | bytes 1990664 | tf_op jit(solution)/shard_map/ppermute | solution.py:100
  88.9 9.1 %collective-permute-start.12 = (f32[2,2,2,162,128]{4,2,3,1,0:T(2,128)S(1)}, f32[2,2,2,162,128]{4,2,3,1,0:T(2,128)S(1)}, u32[]{:S(2)}, u32[]{:S(2)}) collective-permute-start(f32[2,2,2,162,128]{4,2,3,1,0:T(2,128)S(1)} %bitcast.622), channel_id=1, source_target_pairs={{0,16},{16,0},{32,48},{48,32},{64,80},{80,64},{96,112},{112,96},{1... | collective-permute-start | bytes 1990664 | tf_op jit(solution)/shard_map/ppermute | solution.py:100
  89.6 9.4 %collective-permute-start.4 = (f32[2,2,2,162,128]{4,2,3,1,0:T(2,128)S(1)}, f32[2,2,2,162,128]{4,2,3,1,0:T(2,128)S(1)}, u32[]{:S(2)}, u32[]{:S(2)}) collective-permute-start(f32[2,2,2,162,128]{4,2,3,1,0:T(2,128)S(1)} %bitcast.621), channel_id=1, source_target_pairs={{0,16},{16,0},{32,48},{48,32},{64,80},{80,64},{96,112},{112,96},{1... | collective-permute-start | bytes 1990664 | tf_op jit(solution)/shard_map/ppermute | solution.py:100
  95.8 12.2 %collective-permute-start.21 = (f32[2,2,162,128]{3,2,1,0:T(8,128)S(1)}, f32[2,2,162,128]{3,2,1,0:T(8,128)S(1)}, u32[]{:S(2)}, u32[]{:S(2)}) collective-permute-start(f32[2,2,162,128]{3,2,1,0:T(8,128)S(1)} %dynamic-slice_bitcast_fusion), channel_id=1, source_target_pairs={{0,192},{16,208},{32,224},{48,240},{64,128},{80,144},{96,160},{112... | collective-permute-start | bytes 995336 | tf_op jit(solution)/shard_map/ppermute | solution.py:100
  98.1 12.2 %collective-permute-start.13 = (f32[2,2,162,128]{3,2,1,0:T(8,128)S(1)}, f32[2,2,162,128]{3,2,1,0:T(8,128)S(1)}, u32[]{:S(2)}, u32[]{:S(2)}) collective-permute-start(f32[2,2,162,128]{3,2,1,0:T(8,128)S(1)} %dynamic-slice_bitcast_fusion.1), channel_id=1, source_target_pairs={{0,64},{16,80},{32,96},{48,112},{64,0},{80,16},{96,32},{112,48},{1... | collective-permute-start | bytes 995336 | tf_op jit(solution)/shard_map/ppermute | solution.py:100
  99.5 15.2 %collective-permute-start.5 = (f32[2,2,162,128]{3,2,1,0:T(8,128)S(1)}, f32[2,2,162,128]{3,2,1,0:T(8,128)S(1)}, u32[]{:S(2)}, u32[]{:S(2)}) collective-permute-start(f32[2,2,162,128]{3,2,1,0:T(8,128)S(1)} %bitcast.623), channel_id=1, source_target_pairs={{0,192},{16,208},{32,224},{48,240},{64,128},{80,144},{96,160},{112... | collective-permute-start | bytes 995336 | tf_op jit(solution)/shard_map/ppermute | solution.py:100
  108.1 7.4 %collective-permute-start.22 = (f32[2,162,128]{2,1,0:T(8,128)S(1)}, f32[2,162,128]{2,1,0:T(8,128)S(1)}, u32[]{:S(2)}, u32[]{:S(2)}) collective-permute-start(f32[2,162,128]{2,1,0:T(8,128)S(1)} %dynamic-slice_bitcast_fusion.2), channel_id=1, source_target_pairs={{0,32},{16,48},{32,0},{48,16},{64,96},{80,112},{96,64},{112,80},{1... | collective-permute-start | bytes 497672 | tf_op jit(solution)/shard_map/ppermute | solution.py:100
  110.4 7.0 %collective-permute-start.14 = (f32[2,162,128]{2,1,0:T(8,128)S(1)}, f32[2,162,128]{2,1,0:T(8,128)S(1)}, u32[]{:S(2)}, u32[]{:S(2)}) collective-permute-start(f32[2,162,128]{2,1,0:T(8,128)S(1)} %dynamic-slice_bitcast_fusion.3), channel_id=1, source_target_pairs={{0,32},{16,48},{32,0},{48,16},{64,96},{80,112},{96,64},{112,80},{1... | collective-permute-start | bytes 497672 | tf_op jit(solution)/shard_map/ppermute | solution.py:100
  114.9 6.8 %collective-permute-start.6 = (f32[2,162,128]{2,1,0:T(8,128)S(1)}, f32[2,162,128]{2,1,0:T(8,128)S(1)}, u32[]{:S(2)}, u32[]{:S(2)}) collective-permute-start(f32[2,162,128]{2,1,0:T(8,128)S(1)} %dynamic-slice_bitcast_fusion.4), channel_id=1, source_target_pairs={{0,64},{16,80},{32,96},{48,112},{64,0},{80,16},{96,32},{112,48},{1... | collective-permute-start | bytes 497672 | tf_op jit(solution)/shard_map/ppermute | solution.py:100
  115.6 8.3 %collective-permute-start.23 = (f32[162,128]{1,0:T(8,128)S(1)}, f32[162,128]{1,0:T(8,128)S(1)}, u32[]{:S(2)}, u32[]{:S(2)}) collective-permute-start(f32[162,128]{1,0:T(8,128)S(1)} %dynamic-slice_bitcast_fusion.5), channel_id=1, source_target_pairs={{0,64},{16,80},{32,96},{48,112},{64,0},{80,16},{96,32},{112,48},{1... | collective-permute-start | bytes 248840 | tf_op jit(solution)/shard_map/ppermute | solution.py:100
  117.5 6.6 %collective-permute-start.15 = (f32[162,128]{1,0:T(8,128)S(1)}, f32[162,128]{1,0:T(8,128)S(1)}, u32[]{:S(2)}, u32[]{:S(2)}) collective-permute-start(f32[162,128]{1,0:T(8,128)S(1)} %dynamic-slice_bitcast_fusion.6), channel_id=1, source_target_pairs={{0,192},{16,208},{32,224},{48,240},{64,128},{80,144},{96,160},{112... | collective-permute-start | bytes 248840 | tf_op jit(solution)/shard_map/ppermute | solution.py:100
  121.7 6.7 %collective-permute-start.7 = (f32[162,128]{1,0:T(8,128)S(1)}, f32[162,128]{1,0:T(8,128)S(1)}, u32[]{:S(2)}, u32[]{:S(2)}) collective-permute-start(f32[162,128]{1,0:T(8,128)S(1)} %dynamic-slice_bitcast_fusion.7), channel_id=1, source_target_pairs={{0,32},{16,48},{32,0},{48,16},{64,96},{80,112},{96,64},{112,80},{1... | collective-permute-start | bytes 248840 | tf_op jit(solution)/shard_map/ppermute | solution.py:100
  123.9 8.5 %collective-permute-start.24 = (f32[162,128]{1,0:T(8,128)S(1)}, f32[162,128]{1,0:T(8,128)S(1)}, u32[]{:S(2)}, u32[]{:S(2)}) collective-permute-start(f32[162,128]{1,0:T(8,128)S(1)} %bitcast_add_fusion.9), channel_id=1, source_target_pairs={{0,1},{1,0},{2,3},{3,2},{4,5},{5,4},{6,7},{7,6},{8,9},{9,8},{10,11... | collective-permute-start | bytes 248840 | tf_op jit(solution)/shard_map/ppermute | solution.py:110
  124.1 9.3 %collective-permute-start.16 = (f32[162,128]{1,0:T(8,128)S(1)}, f32[162,128]{1,0:T(8,128)S(1)}, u32[]{:S(2)}, u32[]{:S(2)}) collective-permute-start(f32[162,128]{1,0:T(8,128)S(1)} %bitcast_add_fusion.10), channel_id=1, source_target_pairs={{0,3},{1,2},{2,1},{3,0},{4,7},{5,6},{6,5},{7,4},{8,11},{9,10},{10,... | collective-permute-start | bytes 248840 | tf_op jit(solution)/shard_map/ppermute | solution.py:110
  128.4 8.2 %collective-permute-start.8 = (f32[162,128]{1,0:T(8,128)S(1)}, f32[162,128]{1,0:T(8,128)S(1)}, u32[]{:S(2)}, u32[]{:S(2)}) collective-permute-start(f32[162,128]{1,0:T(8,128)S(1)} %bitcast_add_fusion.11), channel_id=1, source_target_pairs={{0,7},{1,6},{2,5},{3,4},{4,3},{5,2},{6,1},{7,0},{8,15},{9,14},{10,... | collective-permute-start | bytes 248840 | tf_op jit(solution)/shard_map/ppermute | solution.py:110
  132.4 6.4 %collective-permute-start.25 = (f32[162,128]{1,0:T(8,128)S(1)}, f32[162,128]{1,0:T(8,128)S(1)}, u32[]{:S(2)}, u32[]{:S(2)}) collective-permute-start(f32[162,128]{1,0:T(8,128)S(1)} %add.480), channel_id=1, source_target_pairs={{0,3},{1,2},{2,1},{3,0},{4,7},{5,6},{6,5},{7,4},{8,11},{9,10},{10,... | collective-permute-start | bytes 248840 | tf_op jit(solution)/shard_map/ppermute | solution.py:110
  133.3 8.7 %collective-permute-start.17 = (f32[162,128]{1,0:T(8,128)S(1)}, f32[162,128]{1,0:T(8,128)S(1)}, u32[]{:S(2)}, u32[]{:S(2)}) collective-permute-start(f32[162,128]{1,0:T(8,128)S(1)} %add.464), channel_id=1, source_target_pairs={{0,7},{1,6},{2,5},{3,4},{4,3},{5,2},{6,1},{7,0},{8,15},{9,14},{10,... | collective-permute-start | bytes 248840 | tf_op jit(solution)/shard_map/ppermute | solution.py:110
  136.6 7.6 %collective-permute-start.9 = (f32[162,128]{1,0:T(8,128)S(1)}, f32[162,128]{1,0:T(8,128)S(1)}, u32[]{:S(2)}, u32[]{:S(2)}) collective-permute-start(f32[162,128]{1,0:T(8,128)S(1)} %add.448), channel_id=1, source_target_pairs={{0,8},{1,9},{2,10},{3,11},{4,12},{5,13},{6,14},{7,15},{8,0},{9,1},... | collective-permute-start | bytes 248840 | tf_op jit(solution)/shard_map/ppermute | solution.py:110
  138.9 6.5 %collective-permute-start.26 = (f32[162,128]{1,0:T(8,128)S(1)}, f32[162,128]{1,0:T(8,128)S(1)}, u32[]{:S(2)}, u32[]{:S(2)}) collective-permute-start(f32[162,128]{1,0:T(8,128)S(1)} %add.481), channel_id=1, source_target_pairs={{0,7},{1,6},{2,5},{3,4},{4,3},{5,2},{6,1},{7,0},{8,15},{9,14},{10,... | collective-permute-start | bytes 248840 | tf_op jit(solution)/shard_map/ppermute | solution.py:110
  142.1 6.1 %collective-permute-start.18 = (f32[162,128]{1,0:T(8,128)S(1)}, f32[162,128]{1,0:T(8,128)S(1)}, u32[]{:S(2)}, u32[]{:S(2)}) collective-permute-start(f32[162,128]{1,0:T(8,128)S(1)} %add.465), channel_id=1, source_target_pairs={{0,8},{1,9},{2,10},{3,11},{4,12},{5,13},{6,14},{7,15},{8,0},{9,1},... | collective-permute-start | bytes 248840 | tf_op jit(solution)/shard_map/ppermute | solution.py:110
  144.2 6.6 %collective-permute-start.10 = (f32[162,128]{1,0:T(8,128)S(1)}, f32[162,128]{1,0:T(8,128)S(1)}, u32[]{:S(2)}, u32[]{:S(2)}) collective-permute-start(f32[162,128]{1,0:T(8,128)S(1)} %add.449), channel_id=1, source_target_pairs={{0,1},{1,0},{2,3},{3,2},{4,5},{5,4},{6,7},{7,6},{8,9},{9,8},{10,11... | collective-permute-start | bytes 248840 | tf_op jit(solution)/shard_map/ppermute | solution.py:110
  145.4 8.0 %collective-permute-start.27 = (f32[162,128]{1,0:T(8,128)S(1)}, f32[162,128]{1,0:T(8,128)S(1)}, u32[]{:S(2)}, u32[]{:S(2)}) collective-permute-start(f32[162,128]{1,0:T(8,128)S(1)} %add.482), channel_id=1, source_target_pairs={{0,8},{1,9},{2,10},{3,11},{4,12},{5,13},{6,14},{7,15},{8,0},{9,1},... | collective-permute-start | bytes 248840 | tf_op jit(solution)/shard_map/ppermute | solution.py:110
  148.2 6.0 %collective-permute-start.19 = (f32[162,128]{1,0:T(8,128)S(1)}, f32[162,128]{1,0:T(8,128)S(1)}, u32[]{:S(2)}, u32[]{:S(2)}) collective-permute-start(f32[162,128]{1,0:T(8,128)S(1)} %add.466), channel_id=1, source_target_pairs={{0,1},{1,0},{2,3},{3,2},{4,5},{5,4},{6,7},{7,6},{8,9},{9,8},{10,11... | collective-permute-start | bytes 248840 | tf_op jit(solution)/shard_map/ppermute | solution.py:110
  150.8 6.4 %collective-permute-start.11 = (f32[162,128]{1,0:T(8,128)S(1)}, f32[162,128]{1,0:T(8,128)S(1)}, u32[]{:S(2)}, u32[]{:S(2)}) collective-permute-start(f32[162,128]{1,0:T(8,128)S(1)} %add.450), channel_id=1, source_target_pairs={{0,3},{1,2},{2,1},{3,0},{4,7},{5,6},{6,5},{7,4},{8,11},{9,10},{10,... | collective-permute-start | bytes 248840 | tf_op jit(solution)/shard_map/ppermute | solution.py:110
  (19 other events, 27.9 us)
